TPU v7x, 256 devices: a whole 4x4x8 slice. The times are simulated.
256 devices in a mesh: cfg: 2 (over core), req: 16 (over x, y), tp: 8 (over z).
Axes of the slice: x: 4, y: 4, z: 8, core: 2. Of those that a mesh axis runs over, the one named last changes fastest.
Arguments:
- latent: float32 [6144, 64], P(('req', 'tp')), may hold values from -6 to 6
- states: float32 [2, 6144, 1536], P('cfg', ('req', 'tp')), may hold values from -12 to 12
- token_counts: int32 [3], replicated, may hold values from 1 to 3840, 6144 in all
- text_lens: int32 [2, 3], P('cfg'), may hold values from 1 to 512, 768 in all within a row
- steps_index: int32 [3], replicated, may hold values from 0 to 49
- modulation: float32 [3, 6, 1536], replicated, may hold values from -3 to 3
- self_qkv: bfloat16 [1536, 3, 2048], P(None, None, 'tp'), may hold values from -0.15625 to 0.15625
- self_out: bfloat16 [2048, 1536], P('tp'), may hold values from -0.15625 to 0.15625
- qk_gains: float32 [4, 2048], P(None, 'tp'), may hold values from 0.8 to 2
- cross_query: bfloat16 [1536, 2048], P(None, 'tp'), may hold values from -1 to 1
- cross_out: bfloat16 [2048, 1536], P('tp'), may hold values from -0.15625 to 0.15625
- cross_gain: float32 [1536], replicated, may hold values from 0.25 to 1.75
- text_kv: bfloat16 [2, 3, 2, 512, 2048], P('cfg', None, None, None, 'tp'), may hold values from -6 to 6
- ffn_in_weight: bfloat16 [8960, 1536], P(('cfg', 'tp')), may hold values from -0.15625 to 0.15625
- ffn_out_weight: bfloat16 [8960, 1536], P(('cfg', 'tp')), may hold values from -0.0625 to 0.0625
- head_weight: bfloat16 [1536, 64], replicated, may hold values from -0.15625 to 0.15625
Outputs:
- new_latent: float32 [6144, 64], P(('req', 'tp'), 'cfg')
- velocity: float32 [6144, 64], P(('req', 'tp'), 'cfg')
- peak: float32 [3], replicated
Inputs may be any that keep to these rules, and one draw needn't show every extreme that they name: `token_counts`: the counts sum to 6144 and the largest is exactly 3840. `text_lens`: in each prompt half the counts sum to 768 and the largest is exactly 512.
All inputs are finite; a program needn't handle non-finite values.
Results may differ from a plain program's by a relative error of at most 0.03.
Values may be sent and summed in bfloat16 or wider, within the bound.
No kernel may reach another device: no remote copies, remote signals or barrier semaphores. Data moves between devices by JAX's collectives and lax.ppermute only.
A program may use at most 64 MiB of HBM per device.

v0:
```python
import jax
import jax.numpy as jnp
import functools
from jax import lax
from jax.experimental import pallas as pl
from jax.sharding import PartitionSpec as P

HEADS = 12
HD = 128
STEPS = 50


key_block = 1024
guide_scale = 5.0
rescale_mix = 0.7
flow_shift = 5.0
norm_eps = 1e-06
stat_eps = 1e-05


def swapped(value, axis, stride):
    mask = 2**stride
    pairs = [(source, source ^ mask) for source in range(lax.axis_size(axis))]
    return lax.ppermute(value, axis, pairs)


def shifted(value, axis, step):
    size = lax.axis_size(axis)
    return lax.ppermute(value, axis, [(source, (source + step) % size) for source in range(size)])


def ring_gather(value, axis):
    size = lax.axis_size(axis)
    forward, backward = value, value
    ahead, behind = [], []
    for unused in range(size // 2):
        forward = shifted(forward, axis, 1)
        behind.append(forward)
    for unused in range((size - 1) // 2):
        backward = shifted(backward, axis, -1)
        ahead.append(backward)
    by_offset = jnp.stack([value] + ahead + behind[::-1])
    doubled = jnp.concatenate([by_offset, by_offset], axis=0)
    start = (size - lax.axis_index(axis)) % size
    ordered = lax.dynamic_slice_in_dim(doubled, start, size, axis=0)
    return ordered.reshape((size * value.shape[0],) + value.shape[1:])


def scatter_sum(value, axis):
    size = lax.axis_size(axis)
    me = lax.axis_index(axis)
    blocks = value.reshape((size, value.shape[0] // size) + value.shape[1:])
    total = lax.dynamic_index_in_dim(blocks, me, 0, keepdims=False).astype(jnp.float32)
    for step in range(1, size):
        outgoing = lax.dynamic_index_in_dim(blocks, (me + step) % size, 0, keepdims=False)
        total = total + shifted(outgoing, axis, step).astype(jnp.float32)
    return total


def butterfly_sum(value, axis):
    stride = 1
    while stride < lax.axis_size(axis):
        value = value + swapped(value, axis, stride.bit_length() - 1)
        stride *= 2
    return value


def layer_norm(values):
    average = jnp.mean(values, axis=-1, keepdims=True)
    centered = values - average
    spread = jnp.mean(centered * centered, axis=-1, keepdims=True)
    return centered * lax.rsqrt(spread + norm_eps)


def rms_scale(values, square_sum, width, gains):
    return (values * lax.rsqrt(square_sum / width + norm_eps)[:, None] * gains).astype(jnp.bfloat16)


def request_of(positions, request_ends):
    return jnp.sum((positions[:, None] >= request_ends[None, :]).astype(jnp.int32), axis=1)


def attention_body(head_count, head_width, q_ref, k_ref, v_ref, qreq_ref, kreq_ref, num_ref, den_ref):
    @pl.when(pl.program_id(0) == 0)
    def _():
        num_ref[...] = jnp.zeros_like(num_ref)
        den_ref[...] = jnp.zeros_like(den_ref)

    same_req = qreq_ref[...] == kreq_ref[...]
    for head in range(head_count):
        cols = slice(head * head_width, (head + 1) * head_width)
        scores = lax.dot_general(
            q_ref[:, cols], k_ref[:, cols], (((1,), (1,)), ((), ())), preferred_element_type=jnp.float32
        ) * head_width ** (-0.5)
        weights = jnp.where(same_req, jnp.exp(scores), 0.0)
        num_ref[:, cols] += jnp.dot(
            weights.astype(jnp.bfloat16), v_ref[:, cols], preferred_element_type=jnp.float32
        )
        den_ref[:, cols] += jnp.broadcast_to(jnp.sum(weights, axis=1, keepdims=True), (weights.shape[0], head_width))


def attention_sums(queries, query_req, key_rows, value_rows, key_req, head_count, head_width, key_block):
    query_count, width = queries.shape
    key_count = key_rows.shape[0]
    steps = key_count // key_block
    flops = 4 * query_count * key_count * width
    return pl.pallas_call(
        functools.partial(attention_body, head_count, head_width),
        grid=(steps,),
        in_specs=[
            pl.BlockSpec((query_count, width), lambda j: (0, 0)),
            pl.BlockSpec((key_block, width), lambda j: (j, 0)),
            pl.BlockSpec((key_block, width), lambda j: (j, 0)),
            pl.BlockSpec((query_count, 1), lambda j: (0, 0)),
            pl.BlockSpec((1, key_block), lambda j: (0, j)),
        ],
        out_specs=[
            pl.BlockSpec((query_count, width), lambda j: (0, 0)),
            pl.BlockSpec((query_count, width), lambda j: (0, 0)),
        ],
        out_shape=[
            jax.ShapeDtypeStruct((query_count, width), jnp.float32),
            jax.ShapeDtypeStruct((query_count, width), jnp.float32),
        ],
        cost_estimate=pl.CostEstimate(
            flops=flops,
            transcendentals=query_count * key_count * head_count,
            bytes_accessed=2 * (query_count + 2 * key_count) * width + 8 * query_count * width,
        ),
    )(queries, key_rows, value_rows, query_req.reshape(query_count, 1), key_req.reshape(1, key_count))


def gather_project(row_block, weight):
    return jnp.dot(ring_gather(row_block, "tp"), weight, preferred_element_type=jnp.float32)


def scatter_project(mixed, weight):
    return scatter_sum(
        jnp.dot(mixed, weight, preferred_element_type=jnp.float32).astype(jnp.bfloat16), "tp"
    )


def feed_forward(ffn_rows, in_weight, out_weight):
    partner_in, partner_out = swapped((in_weight, out_weight), "cfg", 0)
    units = in_weight.shape[0]
    rows = ring_gather(ffn_rows, "tp")
    up_part = lax.dot_general(
        rows,
        jnp.concatenate([in_weight, partner_in], axis=0),
        (((1,), (1,)), ((), ())),
        preferred_element_type=jnp.float32,
    )
    activated = jax.nn.gelu(up_part, approximate=True).astype(jnp.bfloat16)
    own_term = jnp.dot(activated[:, :units], out_weight, preferred_element_type=jnp.float32)
    partner_term = jnp.dot(activated[:, units:], partner_out, preferred_element_type=jnp.float32)
    pair = own_term.astype(jnp.bfloat16).astype(jnp.float32) + partner_term.astype(
        jnp.bfloat16
    ).astype(jnp.float32)
    return scatter_sum(pair.astype(jnp.bfloat16), "tp")


def noise_level(step_value):
    fraction = 1.0 - step_value / STEPS
    return flow_shift * fraction / (1.0 + (flow_shift - 1.0) * fraction)


def shards(
    latent,
    states,
    token_counts,
    text_lens,
    steps_index,
    modulation,
    self_qkv,
    self_out,
    qk_gains,
    cross_query,
    cross_out,
    cross_gain,
    text_kv,
    ffn_in_weight,
    ffn_out_weight,
    head_weight,
):
    row_count = latent.shape[0]
    head_width = HD
    local_cols = self_out.shape[0]
    head_count = local_cols // head_width
    model_width = head_weight.shape[0]
    request_count = token_counts.shape[0]
    tp_parts = lax.axis_size("tp")
    block_rows = row_count * tp_parts
    all_tokens = block_rows * lax.axis_size("req")
    request_ends = jnp.cumsum(token_counts)
    request_range = jnp.arange(request_count, dtype=jnp.int32)
    row_pos = (lax.axis_index("req") * tp_parts + lax.axis_index("tp")) * row_count + jnp.arange(
        row_count, dtype=jnp.int32
    )
    row_onehot = (request_of(row_pos, request_ends)[:, None] == request_range[None, :]).astype(
        jnp.float32
    )
    block_first = lax.axis_index("req") * block_rows
    query_req = request_of(block_first + jnp.arange(block_rows, dtype=jnp.int32), request_ends)
    head_ids = lax.axis_index("tp") * head_count + jnp.arange(head_count, dtype=jnp.int32)
    keep_cols = jnp.repeat((head_ids < HEADS).astype(jnp.float32), head_width)
    hidden_zero = states[0]
    text_local = text_kv[0]
    text_slots = text_local.shape[2]
    text_raw = (
        text_local[:, 0].reshape(request_count * text_slots, local_cols).astype(jnp.float32)
        * keep_cols
    )
    row_mods = jnp.dot(
        row_onehot,
        modulation.reshape(request_count, 6 * model_width),
        precision=lax.Precision.HIGHEST,
    )
    shift_attn = row_mods[:, :model_width]
    scale_attn = row_mods[:, model_width : 2 * model_width]
    gate_attn = row_mods[:, 2 * model_width : 3 * model_width]
    shift_ffn = row_mods[:, 3 * model_width : 4 * model_width]
    scale_ffn = row_mods[:, 4 * model_width : 5 * model_width]
    gate_ffn = row_mods[:, 5 * model_width :]
    normed = (layer_norm(hidden_zero) * (1.0 + scale_attn) + shift_attn).astype(jnp.bfloat16)
    projected = gather_project(normed, self_qkv.reshape(model_width, 3 * local_cols))
    query_raw = projected[:, :local_cols] * keep_cols
    key_raw = projected[:, local_cols : 2 * local_cols] * keep_cols
    norm_sums = butterfly_sum(
        jnp.concatenate(
            [
                jnp.sum(query_raw * query_raw, axis=1),
                jnp.sum(key_raw * key_raw, axis=1),
                jnp.sum(text_raw * text_raw, axis=1),
            ]
        ),
        "tp",
    )
    query_sq = norm_sums[:block_rows]
    key_sq = norm_sums[block_rows : 2 * block_rows]
    text_sq = norm_sums[2 * block_rows :]
    queries = rms_scale(query_raw, query_sq, model_width, qk_gains[0])
    key_rows = rms_scale(key_raw, key_sq, model_width, qk_gains[1])
    value_rows = projected[:, 2 * local_cols :].astype(jnp.bfloat16)
    kv_all = lax.all_gather(jnp.stack([key_rows, value_rows]), "req", axis=1, tiled=True)
    key_all = kv_all[0]
    value_all = kv_all[1]
    key_pos = jnp.arange(all_tokens, dtype=jnp.int32)
    self_num, self_den = attention_sums(
        queries,
        query_req,
        key_all,
        value_all,
        request_of(key_pos, request_ends),
        head_count,
        head_width,
        key_block,
    )
    self_mix = (self_num / self_den * keep_cols).astype(jnp.bfloat16)
    hidden_one = hidden_zero + gate_attn * scatter_project(self_mix, self_out)
    cross_in = (layer_norm(hidden_one) * cross_gain).astype(jnp.bfloat16)
    cross_raw = gather_project(cross_in, cross_query) * keep_cols
    cross_sq = butterfly_sum(jnp.sum(cross_raw * cross_raw, axis=1), "tp")
    cross_q = rms_scale(cross_raw, cross_sq, model_width, qk_gains[2])
    text_keys = rms_scale(text_raw, text_sq, model_width, qk_gains[3])
    text_values = text_local[:, 1].reshape(request_count * text_slots, local_cols)
    text_req = jnp.repeat(request_range, text_slots)
    text_pos = jnp.tile(jnp.arange(text_slots, dtype=jnp.int32), request_count)
    text_limit = jnp.sum(
        jnp.where(text_req[:, None] == request_range[None, :], text_lens[0][None, :], 0), axis=1
    )
    text_req = jnp.where(text_pos < text_limit, text_req, -1)
    cross_num, cross_den = attention_sums(
        cross_q, query_req, text_keys, text_values, text_req, head_count, head_width, text_slots
    )
    cross_mix = (cross_num / cross_den * keep_cols).astype(jnp.bfloat16)
    hidden_two = hidden_one + scatter_project(cross_mix, cross_out)
    ffn_in = (layer_norm(hidden_two) * (1.0 + scale_ffn) + shift_ffn).astype(jnp.bfloat16)
    hidden_three = hidden_two + gate_ffn * feed_forward(ffn_in, ffn_in_weight, ffn_out_weight)
    velocity_own = jnp.dot(
        layer_norm(hidden_three).astype(jnp.bfloat16),
        head_weight,
        preferred_element_type=jnp.float32,
    )
    velocity_other = swapped(velocity_own, "cfg", 0)
    first_half = lax.axis_index("cfg") == 0
    cond_speed = jnp.where(first_half, velocity_own, velocity_other)
    plain_speed = jnp.where(first_half, velocity_other, velocity_own)
    guided = plain_speed + guide_scale * (cond_speed - plain_speed)
    row_squares = jnp.stack(
        [jnp.sum(cond_speed * cond_speed, axis=1), jnp.sum(guided * guided, axis=1)], axis=1
    )
    square_sums = jnp.dot(jnp.transpose(row_onehot), row_squares, precision=lax.Precision.HIGHEST)
    peak_speed = jnp.max(row_onehot * jnp.max(jnp.abs(guided), axis=1)[:, None], axis=0)
    packed = jnp.concatenate([square_sums.reshape(-1), peak_speed])
    sum_count = 2 * request_count
    for axis in ("tp", "req"):
        stride = 1
        while stride < lax.axis_size(axis):
            other = swapped(packed, axis, stride.bit_length() - 1)
            packed = jnp.concatenate(
                [packed[:sum_count] + other[:sum_count], jnp.maximum(packed[sum_count:], other[sum_count:])]
            )
            stride *= 2
    square_sums = packed[:sum_count].reshape(request_count, 2)
    peak_speed = packed[sum_count:]
    entry_counts = token_counts.astype(jnp.float32) * guided.shape[1]
    cond_rms = jnp.sqrt(square_sums[:, 0] / entry_counts + stat_eps)
    guided_rms = jnp.sqrt(square_sums[:, 1] / entry_counts + stat_eps)
    factor = rescale_mix * cond_rms / guided_rms + (1.0 - rescale_mix)
    step_value = steps_index.astype(jnp.float32)
    delta_t = noise_level(step_value + 1.0) - noise_level(step_value)
    per_row = jnp.dot(
        row_onehot, jnp.stack([factor, delta_t], axis=1), precision=lax.Precision.HIGHEST
    )
    velocity = per_row[:, 0:1] * guided
    new_latent = latent + per_row[:, 1:2] * velocity
    own_cols = guided.shape[1] // lax.axis_size("cfg")
    col_start = lax.axis_index("cfg") * own_cols
    velocity_part = lax.dynamic_slice_in_dim(velocity, col_start, own_cols, 1)
    latent_part = lax.dynamic_slice_in_dim(new_latent, col_start, own_cols, 1)
    return (latent_part, velocity_part, factor * peak_speed)


def solution(mesh):
    in_specs = (
        P(("req", "tp"), None),
        P("cfg", ("req", "tp"), None),
        P(),
        P("cfg", None),
        P(),
        P(),
        P(None, None, "tp"),
        P("tp", None),
        P(None, "tp"),
        P(None, "tp"),
        P("tp", None),
        P(),
        P("cfg", None, None, None, "tp"),
        P(("cfg", "tp"), None),
        P(("cfg", "tp"), None),
        P(),
    )
    out_specs = (P(("req", "tp"), "cfg"), P(("req", "tp"), "cfg"), P())
    return jax.shard_map(shards, mesh=mesh, in_specs=in_specs, out_specs=out_specs, check_vma=False)
```

profile of v0, /device:TPU:2, one launch (start us, length us, event | category | flops | bytes accessed | tf_op | source)
XLA Modules:
  0.0 386.5 jit_solution(11062130125981822200)
XLA Ops:
  13.3 5.9 %collective-permute-start = (bf16[48,1536]{1,0:T(8,128)(2,1)S(1)}, bf16[48,1536]{1,0:T(8,128)(2,1)S(1)}, u32[]{:S(2)}, u32[]{:S(2)}) collective-permute-start(bf16[48,1536]{1,0:T(8,128)(2,1)S(1)} %get-tuple-element.38), channel_id=1, source_target_pairs={{0,7},{1,0},{2,1},{3,2},{4,3},{5,4},{6,5},{7,6},{8,15},{9,8},{10,9... | collective-permute-start | bytes 442376 | tf_op jit(solution)/shard_map/ppermute | solution.py:29
  19.1 4.3 %copy.44 = bf16[1536,3,256]{0,2,1:T(8,128)(2,1)} copy(bf16[1536,3,256]{2,0,1:T(8,128)(2,1)} %param.22) | data formatting | bytes 4718592 | tf_op args[6]
  24.9 3.3 collective-permute-start.1
  28.9 2.0 collective-permute-done.1
  30.9 3.7 collective-permute-start.2
  35.3 5.7 %collective-permute-done.5 = bf16[48,1536]{1,0:T(8,128)(2,1)S(1)} collective-permute-done((bf16[48,1536]{1,0:T(8,128)(2,1)S(1)}, bf16[48,1536]{1,0:T(8,128)(2,1)S(1)}, u32[]{:S(2)}, u32[]{:S(2)}) %collective-permute-start.5) | collective-permute-done | bytes 147488 | tf_op jit(solution)/shard_map/ppermute | solution.py:29
  41.6 5.7 %collective-permute-done.6 = bf16[48,1536]{1,0:T(8,128)(2,1)S(1)} collective-permute-done((bf16[48,1536]{1,0:T(8,128)(2,1)S(1)}, bf16[48,1536]{1,0:T(8,128)(2,1)S(1)}, u32[]{:S(2)}, u32[]{:S(2)}) %collective-permute-start.6) | collective-permute-done | bytes 147488 | tf_op jit(solution)/shard_map/ppermute | solution.py:29
  58.1 3.7 collective-permute-done.7
  61.9 4.6 %collective-permute-done.8 = f32[2304]{0:T(1024)S(1)} collective-permute-done((f32[2304]{0:T(1024)S(1)}, f32[2304]{0:T(1024)S(1)}, u32[]{:S(2)}, u32[]{:S(2)}) %collective-permute-start.8) | collective-permute-done | bytes 9248 | tf_op jit(solution)/shard_map/ppermute | solution.py:24
  68.1 6.1 %collective-permute-done.9 = f32[2304]{0:T(1024)S(1)} collective-permute-done((f32[2304]{0:T(1024)S(1)}, f32[2304]{0:T(1024)S(1)}, u32[]{:S(2)}, u32[]{:S(2)}) %collective-permute-start.9) | collective-permute-done | bytes 9248 | tf_op jit(solution)/shard_map/ppermute | solution.py:24
  77.6 62.0 %all-gather.2.cloned.1.call-done = bf16[2,6144,256]{2,1,0:T(8,128)(2,1)} async-done(((bf16[2,384,256]{2,1,0:T(8,128)(2,1)}), bf16[2,6144,256]{2,1,0:T(8,128)(2,1)}) %all-gather.2.cloned.1.call-update) | async-done | bytes 6291472 | tf_op jit(solution)/shard_map/all_gather | solution.py:244
  139.6 5.9 %slice_bitcast_fusion = (bf16[6144,256]{1,0:T(8,128)(2,1)}, bf16[6144,256]{1,0:T(8,128)(2,1)}) fusion(bf16[2,6144,256]{2,1,0:T(8,128)(2,1)} %all-gather.2.cloned.1.call-done), kind=kLoop, calls=%fused_computation.4 | loop fusion | bytes 12582912 | tf_op jit(solution)/shard_map/squeeze | solution.py:246
  145.5 10.4 %shard_map.175 = (f32[384,256]{1,0:T(8,128)}, f32[384,256]{1,0:T(8,128)}) custom-call(bf16[384,256]{1,0:T(8,128)(2,1)} %get-tuple-element.44.q_ref, bf16[6144,256]{1,0:T(8,128)(2,1)} %get-tuple-element.40.k_ref, bf16[6144,256]{1,0:T(8,128)(2,1)} %get-tuple-element.39.v_ref, s32[384,1]{1,0:T(8,128)} %reshape.199.qreq_ref, s32[1,6144]{1,0:T(1,128)} %bitcast.226), custom_call_target="tpu_custom_call" | custom-call | flops 2415919104 | bytes 7274496 | tf_op jit(solution)/shard_map/pallas_call | solution.py:107
  159.3 3.3 collective-permute-start.16
  162.6 2.2 collective-permute-start.15
  166.0 3.9 %collective-permute-start.13 = (bf16[48,1536]{1,0:T(8,128)(2,1)}, bf16[48,1536]{1,0:T(8,128)(2,1)}, u32[]{:S(2)}, u32[]{:S(2)}) collective-permute-start(bf16[48,1536]{1,0:T(8,128)(2,1)} %get-tuple-element.63), channel_id=1, source_target_pairs={{0,4},{1,5},{2,6},{3,7},{4,0},{5,1},{6,2},{7,3},{8,12},{9,13},{10,... | collective-permute-start | bytes 442376 | tf_op jit(solution)/shard_map/ppermute | solution.py:29
  169.9 3.5 collective-permute-start.11
  173.5 3.2 collective-permute-done.15
  176.9 10.9 %collective-permute-done.14 = bf16[48,1536]{1,0:T(8,128)(2,1)} collective-permute-done((bf16[48,1536]{1,0:T(8,128)(2,1)}, bf16[48,1536]{1,0:T(8,128)(2,1)}, u32[]{:S(2)}, u32[]{:S(2)}) %collective-permute-start.14) | collective-permute-done | bytes 147488 | tf_op jit(solution)/shard_map/ppermute | solution.py:29
  189.5 6.1 %collective-permute-done.11 = bf16[48,1536]{1,0:T(8,128)(2,1)} collective-permute-done((bf16[48,1536]{1,0:T(8,128)(2,1)S(1)}, bf16[48,1536]{1,0:T(8,128)(2,1)}, u32[]{:S(2)}, u32[]{:S(2)}) %collective-permute-start.11) | collective-permute-done | bytes 147488 | tf_op jit(solution)/shard_map/ppermute | solution.py:29
  200.9 2.5 collective-permute-done.17
  203.4 2.6 collective-permute-start.18
  206.0 2.7 collective-permute-done.18
  208.7 4.1 %collective-permute-start.19 = (bf16[48,1536]{1,0:T(8,128)(2,1)S(1)}, bf16[48,1536]{1,0:T(8,128)(2,1)S(1)}, u32[]{:S(2)}, u32[]{:S(2)}) collective-permute-start(bf16[48,1536]{1,0:T(8,128)(2,1)S(1)} %collective-permute-done.18), channel_id=1, source_target_pairs={{0,7},{1,0},{2,1},{3,2},{4,3},{5,4},{6,5},{7,6},{8,15},{9,8},{10,9... | collective-permute-start | bytes 442376 | tf_op jit(solution)/shard_map/ppermute | solution.py:29
  212.8 7.9 %collective-permute-done.22 = bf16[48,1536]{1,0:T(8,128)(2,1)S(1)} collective-permute-done((bf16[48,1536]{1,0:T(8,128)(2,1)S(1)}, bf16[48,1536]{1,0:T(8,128)(2,1)S(1)}, u32[]{:S(2)}, u32[]{:S(2)}) %collective-permute-start.22) | collective-permute-done | bytes 147488 | tf_op jit(solution)/shard_map/ppermute | solution.py:29
  220.7 6.3 %collective-permute-done.23 = bf16[48,1536]{1,0:T(8,128)(2,1)S(1)} collective-permute-done((bf16[48,1536]{1,0:T(8,128)(2,1)S(1)}, bf16[48,1536]{1,0:T(8,128)(2,1)S(1)}, u32[]{:S(2)}, u32[]{:S(2)}) %collective-permute-start.23) | collective-permute-done | bytes 147488 | tf_op jit(solution)/shard_map/ppermute | solution.py:29
  229.9 2.5 collective-permute-done.24
  232.4 4.5 %collective-permute-done.25 = f32[384]{0:T(512)S(1)} collective-permute-done((f32[384]{0:T(512)S(1)}, f32[384]{0:T(512)S(1)}, u32[]{:S(2)}, u32[]{:S(2)}) %collective-permute-start.25) | collective-permute-done | bytes 1568 | tf_op jit(solution)/shard_map/ppermute | solution.py:24
  238.1 6.3 %collective-permute-done.26 = f32[384]{0:T(512)S(1)} collective-permute-done((f32[384]{0:T(512)S(1)}, f32[384]{0:T(512)S(1)}, u32[]{:S(2)}, u32[]{:S(2)}) %collective-permute-start.26) | collective-permute-done | bytes 1568 | tf_op jit(solution)/shard_map/ppermute | solution.py:24
  245.2 4.8 %shard_map.176 = (f32[384,256]{1,0:T(8,128)}, f32[384,256]{1,0:T(8,128)}) custom-call(bf16[384,256]{1,0:T(8,128)(2,1)} %multiply_convert_fusion.1.q_ref, bf16[1536,256]{1,0:T(8,128)(2,1)} %fusion.22.k_ref, bf16[1536,256]{1,0:T(8,128)(2,1)} %bitcast.223, s32[384,1]{1,0:T(8,128)} %reshape.199.qreq_ref, s32[1,1536]{1,0:T(1,128)} %compare_select_fusion.kreq_ref), custom_call_target="tpu_custom_call" | custom-call | flops 603979776 | bytes 2555904 | tf_op jit(solution)/shard_map/pallas_call | solution.py:107
  250.0 1.8 convolution_convert_fusion.2
  252.1 4.0 %collective-permute-start.31 = (bf16[48,1536]{1,0:T(8,128)(2,1)S(1)}, bf16[48,1536]{1,0:T(8,128)(2,1)S(1)}, u32[]{:S(2)}, u32[]{:S(2)}) collective-permute-start(bf16[48,1536]{1,0:T(8,128)(2,1)S(1)} %get-tuple-element.55), channel_id=1, source_target_pairs={{0,5},{1,6},{2,7},{3,0},{4,1},{5,2},{6,3},{7,4},{8,13},{9,14},{10,... | collective-permute-start | bytes 442376 | tf_op jit(solution)/shard_map/ppermute | solution.py:29
  256.2 2.4 collective-permute-start.30
  258.5 2.4 collective-permute-start.29
  262.1 1.8 collective-permute-done.32
  265.2 3.4 collective-permute-done.30
  268.6 6.1 %collective-permute-done.29 = bf16[48,1536]{1,0:T(8,128)(2,1)S(1)} collective-permute-done((bf16[48,1536]{1,0:T(8,128)(2,1)S(1)}, bf16[48,1536]{1,0:T(8,128)(2,1)S(1)}, u32[]{:S(2)}, u32[]{:S(2)}) %collective-permute-start.29) | collective-permute-done | bytes 147488 | tf_op jit(solution)/shard_map/ppermute | solution.py:29
  274.7 1.8 collective-permute-done.27
  277.5 1.8 collective-permute-start.37
  279.9 2.4 collective-permute-done.34
  284.7 3.4 collective-permute-done.35
  288.1 2.1 collective-permute-start.36
  290.6 7.6 %collective-permute-done.39 = bf16[48,1536]{1,0:T(8,128)(2,1)S(1)} collective-permute-done((bf16[48,1536]{1,0:T(8,128)(2,1)S(1)}, bf16[48,1536]{1,0:T(8,128)(2,1)S(1)}, u32[]{:S(2)}, u32[]{:S(2)}) %collective-permute-start.39) | collective-permute-done | bytes 147488 | tf_op jit(solution)/shard_map/ppermute | solution.py:29
  298.2 6.3 %collective-permute-done.40 = bf16[48,1536]{1,0:T(8,128)(2,1)S(1)} collective-permute-done((bf16[48,1536]{1,0:T(8,128)(2,1)S(1)}, bf16[48,1536]{1,0:T(8,128)(2,1)S(1)}, u32[]{:S(2)}, u32[]{:S(2)}) %collective-permute-start.40) | collective-permute-done | bytes 147488 | tf_op jit(solution)/shard_map/ppermute | solution.py:29
  304.9 2.2 fusion.17
  309.6 3.4 collective-permute-start.48
  312.9 2.7 collective-permute-start.47
  316.1 3.6 collective-permute-start.45
  319.6 2.5 collective-permute-done.49
  323.3 3.0 collective-permute-start.43
  326.3 1.7 collective-permute-done.47
  327.9 2.0 collective-permute-done.46
  329.9 2.6 collective-permute-done.45
  332.5 6.5 %collective-permute-done.44 = bf16[48,1536]{1,0:T(8,128)(2,1)S(1)} collective-permute-done((bf16[48,1536]{1,0:T(8,128)(2,1)S(1)}, bf16[48,1536]{1,0:T(8,128)(2,1)S(1)}, u32[]{:S(2)}, u32[]{:S(2)}) %collective-permute-start.44) | collective-permute-done | bytes 147488 | tf_op jit(solution)/shard_map/ppermute | solution.py:29
  343.2 3.6 collective-permute-done.51
  347.1 4.3 %collective-permute-done.52 = f32[9]{0:T(128)S(1)} collective-permute-done((f32[9]{0:T(128)S(1)}, f32[9]{0:T(128)S(1)}, u32[]{:S(2)}, u32[]{:S(2)}) %collective-permute-start.52) | collective-permute-done | bytes 68 | tf_op jit(solution)/shard_map/ppermute | solution.py:24
  351.5 2.2 collective-permute-start.53
  353.9 5.1 %collective-permute-done.53 = f32[9]{0:T(128)S(1)} collective-permute-done((f32[9]{0:T(128)S(1)}, f32[9]{0:T(128)S(1)}, u32[]{:S(2)}, u32[]{:S(2)}) %collective-permute-start.53) | collective-permute-done | bytes 68 | tf_op jit(solution)/shard_map/ppermute | solution.py:24
  359.6 3.2 collective-permute-done.54
  362.9 1.7 collective-permute-start.55
  364.9 3.2 collective-permute-done.55
  368.9 2.8 collective-permute-done.56
  371.9 2.1 collective-permute-start.57
  374.2 2.8 collective-permute-done.57
  (252 shorter events, 62.6 us)
Async XLA Ops:
  7.2 148.7 %copy-start = (bf16[256,1536]{1,0:T(8,128)(2,1)S(1)}, bf16[256,1536]{1,0:T(8,128)(2,1)}, u32[]{:S(2)}) copy-start(bf16[256,1536]{1,0:T(8,128)(2,1)} %param.23) | copy-start | bytes 2359300
  7.2 132.4 %all-gather.2.cloned.1.call-start = ((), (), s32[]{:S(2)}) async-start(), calls=%async_computation | async-start | bytes 6684672 | tf_op jit(solution)/shard_map/all_gather | solution.py:244
  13.3 11.7 %collective-permute-start = (bf16[48,1536]{1,0:T(8,128)(2,1)S(1)}, bf16[48,1536]{1,0:T(8,128)(2,1)S(1)}, u32[]{:S(2)}, u32[]{:S(2)}) collective-permute-start(bf16[48,1536]{1,0:T(8,128)(2,1)S(1)} %get-tuple-element.38), channel_id=1, source_target_pairs={{0,7},{1,0},{2,1},{3,2},{4,3},{5,4},{6,5},{7,6},{8,15},{9,8},{10,9... | collective-permute-start | bytes 442376 | tf_op jit(solution)/shard_map/ppermute | solution.py:29
  19.1 9.1 %collective-permute-start.3 = (bf16[48,1536]{1,0:T(8,128)(2,1)S(1)}, bf16[48,1536]{1,0:T(8,128)(2,1)S(1)}, u32[]{:S(2)}, u32[]{:S(2)}) collective-permute-start(bf16[48,1536]{1,0:T(8,128)(2,1)S(1)} %get-tuple-element.38), channel_id=1, source_target_pairs={{0,1},{1,2},{2,3},{3,4},{4,5},{5,6},{6,7},{7,0},{8,9},{9,10},{10,1... | collective-permute-start | bytes 442376 | tf_op jit(solution)/shard_map/ppermute | solution.py:29
  24.9 6.0 %collective-permute-start.1 = (bf16[48,1536]{1,0:T(8,128)(2,1)S(1)}, bf16[48,1536]{1,0:T(8,128)(2,1)S(1)}, u32[]{:S(2)}, u32[]{:S(2)}) collective-permute-start(bf16[48,1536]{1,0:T(8,128)(2,1)S(1)} %collective-permute-done), channel_id=1, source_target_pairs={{0,7},{1,0},{2,1},{3,2},{4,3},{5,4},{6,5},{7,6},{8,15},{9,8},{10,9... | collective-permute-start | bytes 442376 | tf_op jit(solution)/shard_map/ppermute | solution.py:29
  28.2 6.4 %collective-permute-start.4 = (bf16[48,1536]{1,0:T(8,128)(2,1)S(1)}, bf16[48,1536]{1,0:T(8,128)(2,1)S(1)}, u32[]{:S(2)}, u32[]{:S(2)}) collective-permute-start(bf16[48,1536]{1,0:T(8,128)(2,1)S(1)} %collective-permute-done.3), channel_id=1, source_target_pairs={{0,1},{1,2},{2,3},{3,4},{4,5},{5,6},{6,7},{7,0},{8,9},{9,10},{10,1... | collective-permute-start | bytes 442376 | tf_op jit(solution)/shard_map/ppermute | solution.py:29
  30.9 10.0 %collective-permute-start.2 = (bf16[48,1536]{1,0:T(8,128)(2,1)S(1)}, bf16[48,1536]{1,0:T(8,128)(2,1)S(1)}, u32[]{:S(2)}, u32[]{:S(2)}) collective-permute-start(bf16[48,1536]{1,0:T(8,128)(2,1)S(1)} %collective-permute-done.1), channel_id=1, source_target_pairs={{0,7},{1,0},{2,1},{3,2},{4,3},{5,4},{6,5},{7,6},{8,15},{9,8},{10,9... | collective-permute-start | bytes 442376 | tf_op jit(solution)/shard_map/ppermute | solution.py:29
  34.6 6.4 %collective-permute-start.5 = (bf16[48,1536]{1,0:T(8,128)(2,1)S(1)}, bf16[48,1536]{1,0:T(8,128)(2,1)S(1)}, u32[]{:S(2)}, u32[]{:S(2)}) collective-permute-start(bf16[48,1536]{1,0:T(8,128)(2,1)S(1)} %collective-permute-done.4), channel_id=1, source_target_pairs={{0,1},{1,2},{2,3},{3,4},{4,5},{5,6},{6,7},{7,0},{8,9},{9,10},{10,1... | collective-permute-start | bytes 442376 | tf_op jit(solution)/shard_map/ppermute | solution.py:29
  41.0 6.4 %collective-permute-start.6 = (bf16[48,1536]{1,0:T(8,128)(2,1)S(1)}, bf16[48,1536]{1,0:T(8,128)(2,1)S(1)}, u32[]{:S(2)}, u32[]{:S(2)}) collective-permute-start(bf16[48,1536]{1,0:T(8,128)(2,1)S(1)} %collective-permute-done.5), channel_id=1, source_target_pairs={{0,1},{1,2},{2,3},{3,4},{4,5},{5,6},{6,7},{7,0},{8,9},{9,10},{10,1... | collective-permute-start | bytes 442376 | tf_op jit(solution)/shard_map/ppermute | solution.py:29
  58.0 3.8 collective-permute-start.7
  61.8 4.7 %collective-permute-start.8 = (f32[2304]{0:T(1024)S(1)}, f32[2304]{0:T(1024)S(1)}, u32[]{:S(2)}, u32[]{:S(2)}) collective-permute-start(f32[2304]{0:T(1024)S(1)} %fusion.74), channel_id=1, source_target_pairs={{0,2},{1,3},{2,0},{3,1},{4,6},{5,7},{6,4},{7,5},{8,10},{9,11},{10,... | collective-permute-start | bytes 27656 | tf_op jit(solution)/shard_map/ppermute | solution.py:24
  66.5 7.8 %collective-permute-start.9 = (f32[2304]{0:T(1024)S(1)}, f32[2304]{0:T(1024)S(1)}, u32[]{:S(2)}, u32[]{:S(2)}) collective-permute-start(f32[2304]{0:T(1024)S(1)} %add.391), channel_id=1, source_target_pairs={{0,4},{1,5},{2,6},{3,7},{4,0},{5,1},{6,2},{7,3},{8,12},{9,13},{10,... | collective-permute-start | bytes 27656 | tf_op jit(solution)/shard_map/ppermute | solution.py:24
  157.5 40.6 %copy-start.7 = (f32[1536]{0:T(1024)S(1)}, f32[1536]{0:T(1024)}, u32[]{:S(2)}) copy-start(f32[1536]{0:T(1024)} %param.27) | copy-start | bytes 18436
  159.3 10.6 %collective-permute-start.16 = (bf16[48,1536]{1,0:T(8,128)(2,1)S(1)}, bf16[48,1536]{1,0:T(8,128)(2,1)S(1)}, u32[]{:S(2)}, u32[]{:S(2)}) collective-permute-start(bf16[48,1536]{1,0:T(8,128)(2,1)S(1)} %get-tuple-element.60), channel_id=1, source_target_pairs={{0,7},{1,0},{2,1},{3,2},{4,3},{5,4},{6,5},{7,6},{8,15},{9,8},{10,9... | collective-permute-start | bytes 442376 | tf_op jit(solution)/shard_map/ppermute | solution.py:29
  162.6 14.1 %collective-permute-start.15 = (bf16[48,1536]{1,0:T(8,128)(2,1)S(1)}, bf16[48,1536]{1,0:T(8,128)(2,1)S(1)}, u32[]{:S(2)}, u32[]{:S(2)}) collective-permute-start(bf16[48,1536]{1,0:T(8,128)(2,1)S(1)} %get-tuple-element.61), channel_id=1, source_target_pairs={{0,6},{1,7},{2,0},{3,1},{4,2},{5,3},{6,4},{7,5},{8,14},{9,15},{10,... | collective-permute-start | bytes 442376 | tf_op jit(solution)/shard_map/ppermute | solution.py:29
  164.8 23.0 %collective-permute-start.14 = (bf16[48,1536]{1,0:T(8,128)(2,1)}, bf16[48,1536]{1,0:T(8,128)(2,1)}, u32[]{:S(2)}, u32[]{:S(2)}) collective-permute-start(bf16[48,1536]{1,0:T(8,128)(2,1)} %get-tuple-element.62), channel_id=1, source_target_pairs={{0,5},{1,6},{2,7},{3,0},{4,1},{5,2},{6,3},{7,4},{8,13},{9,14},{10,... | collective-permute-start | bytes 442376 | tf_op jit(solution)/shard_map/ppermute | solution.py:29
  166.0 21.8 %collective-permute-start.13 = (bf16[48,1536]{1,0:T(8,128)(2,1)}, bf16[48,1536]{1,0:T(8,128)(2,1)}, u32[]{:S(2)}, u32[]{:S(2)}) collective-permute-start(bf16[48,1536]{1,0:T(8,128)(2,1)} %get-tuple-element.63), channel_id=1, source_target_pairs={{0,4},{1,5},{2,6},{3,7},{4,0},{5,1},{6,2},{7,3},{8,12},{9,13},{10,... | collective-permute-start | bytes 442376 | tf_op jit(solution)/shard_map/ppermute | solution.py:29
  169.9 19.5 %collective-permute-start.12 = (bf16[48,1536]{1,0:T(8,128)(2,1)}, bf16[48,1536]{1,0:T(8,128)(2,1)}, u32[]{:S(2)}, u32[]{:S(2)}) collective-permute-start(bf16[48,1536]{1,0:T(8,128)(2,1)} %get-tuple-element.64), channel_id=1, source_target_pairs={{0,3},{1,4},{2,5},{3,6},{4,7},{5,0},{6,1},{7,2},{8,11},{9,12},{10,... | collective-permute-start | bytes 442376 | tf_op jit(solution)/shard_map/ppermute | solution.py:29
  169.9 25.6 %collective-permute-start.11 = (bf16[48,1536]{1,0:T(8,128)(2,1)S(1)}, bf16[48,1536]{1,0:T(8,128)(2,1)}, u32[]{:S(2)}, u32[]{:S(2)}) collective-permute-start(bf16[48,1536]{1,0:T(8,128)(2,1)S(1)} %get-tuple-element.65), channel_id=1, source_target_pairs={{0,2},{1,3},{2,4},{3,5},{4,6},{5,7},{6,0},{7,1},{8,10},{9,11},{10,... | collective-permute-start | bytes 442376 | tf_op jit(solution)/shard_map/ppermute | solution.py:29
  176.7 19.6 %collective-permute-start.10 = (bf16[48,1536]{1,0:T(8,128)(2,1)S(1)}, bf16[48,1536]{1,0:T(8,128)(2,1)}, u32[]{:S(2)}, u32[]{:S(2)}) collective-permute-start(bf16[48,1536]{1,0:T(8,128)(2,1)S(1)} %get-tuple-element.59), channel_id=1, source_target_pairs={{0,1},{1,2},{2,3},{3,4},{4,5},{5,6},{6,7},{7,0},{8,9},{9,10},{10,1... | collective-permute-start | bytes 442376 | tf_op jit(solution)/shard_map/ppermute | solution.py:29
  198.2 5.2 %collective-permute-start.17 = (bf16[48,1536]{1,0:T(8,128)(2,1)S(1)}, bf16[48,1536]{1,0:T(8,128)(2,1)S(1)}, u32[]{:S(2)}, u32[]{:S(2)}) collective-permute-start(bf16[48,1536]{1,0:T(8,128)(2,1)S(1)} %get-tuple-element.34), channel_id=1, source_target_pairs={{0,7},{1,0},{2,1},{3,2},{4,3},{5,4},{6,5},{7,6},{8,15},{9,8},{10,9... | collective-permute-start | bytes 442376 | tf_op jit(solution)/shard_map/ppermute | solution.py:29
  199.7 6.4 %collective-permute-start.20 = (bf16[48,1536]{1,0:T(8,128)(2,1)S(1)}, bf16[48,1536]{1,0:T(8,128)(2,1)S(1)}, u32[]{:S(2)}, u32[]{:S(2)}) collective-permute-start(bf16[48,1536]{1,0:T(8,128)(2,1)S(1)} %get-tuple-element.34), channel_id=1, source_target_pairs={{0,1},{1,2},{2,3},{3,4},{4,5},{5,6},{6,7},{7,0},{8,9},{9,10},{10,1... | collective-permute-start | bytes 442376 | tf_op jit(solution)/shard_map/ppermute | solution.py:29
  203.4 5.3 %collective-permute-start.18 = (bf16[48,1536]{1,0:T(8,128)(2,1)S(1)}, bf16[48,1536]{1,0:T(8,128)(2,1)S(1)}, u32[]{:S(2)}, u32[]{:S(2)}) collective-permute-start(bf16[48,1536]{1,0:T(8,128)(2,1)S(1)} %collective-permute-done.17), channel_id=1, source_target_pairs={{0,7},{1,0},{2,1},{3,2},{4,3},{5,4},{6,5},{7,6},{8,15},{9,8},{10,9... | collective-permute-start | bytes 442376 | tf_op jit(solution)/shard_map/ppermute | solution.py:29
  206.0 6.7 %collective-permute-start.21 = (bf16[48,1536]{1,0:T(8,128)(2,1)S(1)}, bf16[48,1536]{1,0:T(8,128)(2,1)S(1)}, u32[]{:S(2)}, u32[]{:S(2)}) collective-permute-start(bf16[48,1536]{1,0:T(8,128)(2,1)S(1)} %collective-permute-done.20), channel_id=1, source_target_pairs={{0,1},{1,2},{2,3},{3,4},{4,5},{5,6},{6,7},{7,0},{8,9},{9,10},{10,1... | collective-permute-start | bytes 442376 | tf_op jit(solution)/shard_map/ppermute | solution.py:29
  208.7 12.0 %collective-permute-start.19 = (bf16[48,1536]{1,0:T(8,128)(2,1)S(1)}, bf16[48,1536]{1,0:T(8,128)(2,1)S(1)}, u32[]{:S(2)}, u32[]{:S(2)}) collective-permute-start(bf16[48,1536]{1,0:T(8,128)(2,1)S(1)} %collective-permute-done.18), channel_id=1, source_target_pairs={{0,7},{1,0},{2,1},{3,2},{4,3},{5,4},{6,5},{7,6},{8,15},{9,8},{10,9... | collective-permute-start | bytes 442376 | tf_op jit(solution)/shard_map/ppermute | solution.py:29
  212.8 7.9 %collective-permute-start.22 = (bf16[48,1536]{1,0:T(8,128)(2,1)S(1)}, bf16[48,1536]{1,0:T(8,128)(2,1)S(1)}, u32[]{:S(2)}, u32[]{:S(2)}) collective-permute-start(bf16[48,1536]{1,0:T(8,128)(2,1)S(1)} %collective-permute-done.21), channel_id=1, source_target_pairs={{0,1},{1,2},{2,3},{3,4},{4,5},{5,6},{6,7},{7,0},{8,9},{9,10},{10,1... | collective-permute-start | bytes 442376 | tf_op jit(solution)/shard_map/ppermute | solution.py:29
  220.6 6.4 %collective-permute-start.23 = (bf16[48,1536]{1,0:T(8,128)(2,1)S(1)}, bf16[48,1536]{1,0:T(8,128)(2,1)S(1)}, u32[]{:S(2)}, u32[]{:S(2)}) collective-permute-start(bf16[48,1536]{1,0:T(8,128)(2,1)S(1)} %collective-permute-done.22), channel_id=1, source_target_pairs={{0,1},{1,2},{2,3},{3,4},{4,5},{5,6},{6,7},{7,0},{8,9},{9,10},{10,1... | collective-permute-start | bytes 442376 | tf_op jit(solution)/shard_map/ppermute | solution.py:29
  228.8 3.7 collective-permute-start.24
  232.4 4.5 %collective-permute-start.25 = (f32[384]{0:T(512)S(1)}, f32[384]{0:T(512)S(1)}, u32[]{:S(2)}, u32[]{:S(2)}) collective-permute-start(f32[384]{0:T(512)S(1)} %add.428), channel_id=1, source_target_pairs={{0,2},{1,3},{2,0},{3,1},{4,6},{5,7},{6,4},{7,5},{8,10},{9,11},{10,... | collective-permute-start | bytes 4616 | tf_op jit(solution)/shard_map/ppermute | solution.py:24
  236.9 7.5 %collective-permute-start.26 = (f32[384]{0:T(512)S(1)}, f32[384]{0:T(512)S(1)}, u32[]{:S(2)}, u32[]{:S(2)}) collective-permute-start(f32[384]{0:T(512)S(1)} %add.429), channel_id=1, source_target_pairs={{0,4},{1,5},{2,6},{3,7},{4,0},{5,1},{6,2},{7,3},{8,12},{9,13},{10,... | collective-permute-start | bytes 4616 | tf_op jit(solution)/shard_map/ppermute | solution.py:24
  252.0 8.9 %collective-permute-start.33 = (bf16[48,1536]{1,0:T(8,128)(2,1)S(1)}, bf16[48,1536]{1,0:T(8,128)(2,1)S(1)}, u32[]{:S(2)}, u32[]{:S(2)}) collective-permute-start(bf16[48,1536]{1,0:T(8,128)(2,1)S(1)} %get-tuple-element.53), channel_id=1, source_target_pairs={{0,7},{1,0},{2,1},{3,2},{4,3},{5,4},{6,5},{7,6},{8,15},{9,8},{10,9... | collective-permute-start | bytes 442376 | tf_op jit(solution)/shard_map/ppermute | solution.py:29
  252.0 11.9 %collective-permute-start.32 = (bf16[48,1536]{1,0:T(8,128)(2,1)S(1)}, bf16[48,1536]{1,0:T(8,128)(2,1)S(1)}, u32[]{:S(2)}, u32[]{:S(2)}) collective-permute-start(bf16[48,1536]{1,0:T(8,128)(2,1)S(1)} %get-tuple-element.54), channel_id=1, source_target_pairs={{0,6},{1,7},{2,0},{3,1},{4,2},{5,3},{6,4},{7,5},{8,14},{9,15},{10,... | collective-permute-start | bytes 442376 | tf_op jit(solution)/shard_map/ppermute | solution.py:29
  252.1 13.0 %collective-permute-start.31 = (bf16[48,1536]{1,0:T(8,128)(2,1)S(1)}, bf16[48,1536]{1,0:T(8,128)(2,1)S(1)}, u32[]{:S(2)}, u32[]{:S(2)}) collective-permute-start(bf16[48,1536]{1,0:T(8,128)(2,1)S(1)} %get-tuple-element.55), channel_id=1, source_target_pairs={{0,5},{1,6},{2,7},{3,0},{4,1},{5,2},{6,3},{7,4},{8,13},{9,14},{10,... | collective-permute-start | bytes 442376 | tf_op jit(solution)/shard_map/ppermute | solution.py:29
  256.2 12.4 %collective-permute-start.30 = (bf16[48,1536]{1,0:T(8,128)(2,1)S(1)}, bf16[48,1536]{1,0:T(8,128)(2,1)S(1)}, u32[]{:S(2)}, u32[]{:S(2)}) collective-permute-start(bf16[48,1536]{1,0:T(8,128)(2,1)S(1)} %get-tuple-element.56), channel_id=1, source_target_pairs={{0,4},{1,5},{2,6},{3,7},{4,0},{5,1},{6,2},{7,3},{8,12},{9,13},{10,... | collective-permute-start | bytes 442376 | tf_op jit(solution)/shard_map/ppermute | solution.py:29
  258.5 16.1 %collective-permute-start.29 = (bf16[48,1536]{1,0:T(8,128)(2,1)S(1)}, bf16[48,1536]{1,0:T(8,128)(2,1)S(1)}, u32[]{:S(2)}, u32[]{:S(2)}) collective-permute-start(bf16[48,1536]{1,0:T(8,128)(2,1)S(1)} %get-tuple-element.57), channel_id=1, source_target_pairs={{0,3},{1,4},{2,5},{3,6},{4,7},{5,0},{6,1},{7,2},{8,11},{9,12},{10,... | collective-permute-start | bytes 442376 | tf_op jit(solution)/shard_map/ppermute | solution.py:29
  260.9 13.8 %collective-permute-start.28 = (bf16[48,1536]{1,0:T(8,128)(2,1)S(1)}, bf16[48,1536]{1,0:T(8,128)(2,1)S(1)}, u32[]{:S(2)}, u32[]{:S(2)}) collective-permute-start(bf16[48,1536]{1,0:T(8,128)(2,1)S(1)} %get-tuple-element.58), channel_id=1, source_target_pairs={{0,2},{1,3},{2,4},{3,5},{4,6},{5,7},{6,0},{7,1},{8,10},{9,11},{10,... | collective-permute-start | bytes 442376 | tf_op jit(solution)/shard_map/ppermute | solution.py:29
  263.9 12.5 %collective-permute-start.27 = (bf16[48,1536]{1,0:T(8,128)(2,1)S(1)}, bf16[48,1536]{1,0:T(8,128)(2,1)S(1)}, u32[]{:S(2)}, u32[]{:S(2)}) collective-permute-start(bf16[48,1536]{1,0:T(8,128)(2,1)S(1)} %get-tuple-element.52), channel_id=1, source_target_pairs={{0,1},{1,2},{2,3},{3,4},{4,5},{5,6},{6,7},{7,0},{8,9},{9,10},{10,1... | collective-permute-start | bytes 442376 | tf_op jit(solution)/shard_map/ppermute | solution.py:29
  277.1 5.2 %collective-permute-start.34 = (bf16[48,1536]{1,0:T(8,128)(2,1)S(1)}, bf16[48,1536]{1,0:T(8,128)(2,1)S(1)}, u32[]{:S(2)}, u32[]{:S(2)}) collective-permute-start(bf16[48,1536]{1,0:T(8,128)(2,1)S(1)} %get-tuple-element.30), channel_id=1, source_target_pairs={{0,7},{1,0},{2,1},{3,2},{4,3},{5,4},{6,5},{7,6},{8,15},{9,8},{10,9... | collective-permute-start | bytes 442376 | tf_op jit(solution)/shard_map/ppermute | solution.py:29
  277.5 6.5 %collective-permute-start.37 = (bf16[48,1536]{1,0:T(8,128)(2,1)S(1)}, bf16[48,1536]{1,0:T(8,128)(2,1)S(1)}, u32[]{:S(2)}, u32[]{:S(2)}) collective-permute-start(bf16[48,1536]{1,0:T(8,128)(2,1)S(1)} %get-tuple-element.30), channel_id=1, source_target_pairs={{0,1},{1,2},{2,3},{3,4},{4,5},{5,6},{6,7},{7,0},{8,9},{9,10},{10,1... | collective-permute-start | bytes 442376 | tf_op jit(solution)/shard_map/ppermute | solution.py:29
  279.3 25.5 %collective-permute-start.41 = (bf16[560,1536]{1,0:T(8,128)(2,1)S(1)}, bf16[560,1536]{1,0:T(8,128)(2,1)S(1)}, u32[]{:S(2)}, u32[]{:S(2)}) collective-permute-start(bf16[560,1536]{1,0:T(8,128)(2,1)S(1)} %copy-done.11), channel_id=1, source_target_pairs={{0,128},{128,0},{1,129},{129,1},{2,130},{130,2},{3,131},{131,3},{4... | collective-permute-start | bytes 5160968 | tf_op jit(solution)/shard_map/ppermute | solution.py:24
  279.4 28.8 %collective-permute-start.42 = (bf16[560,1536]{1,0:T(8,128)(2,1)S(1)}, bf16[560,1536]{1,0:T(8,128)(2,1)S(1)}, u32[]{:S(2)}, u32[]{:S(2)}) collective-permute-start(bf16[560,1536]{1,0:T(8,128)(2,1)S(1)} %copy-done.12), channel_id=1, source_target_pairs={{0,128},{128,0},{1,129},{129,1},{2,130},{130,2},{3,131},{131,3},{4... | collective-permute-start | bytes 5160968 | tf_op jit(solution)/shard_map/ppermute | solution.py:24
  282.3 5.8 %collective-permute-start.35 = (bf16[48,1536]{1,0:T(8,128)(2,1)S(1)}, bf16[48,1536]{1,0:T(8,128)(2,1)S(1)}, u32[]{:S(2)}, u32[]{:S(2)}) collective-permute-start(bf16[48,1536]{1,0:T(8,128)(2,1)S(1)} %collective-permute-done.34), channel_id=1, source_target_pairs={{0,7},{1,0},{2,1},{3,2},{4,3},{5,4},{6,5},{7,6},{8,15},{9,8},{10,9... | collective-permute-start | bytes 442376 | tf_op jit(solution)/shard_map/ppermute | solution.py:29
  284.1 6.5 %collective-permute-start.38 = (bf16[48,1536]{1,0:T(8,128)(2,1)S(1)}, bf16[48,1536]{1,0:T(8,128)(2,1)S(1)}, u32[]{:S(2)}, u32[]{:S(2)}) collective-permute-start(bf16[48,1536]{1,0:T(8,128)(2,1)S(1)} %collective-permute-done.37), channel_id=1, source_target_pairs={{0,1},{1,2},{2,3},{3,4},{4,5},{5,6},{6,7},{7,0},{8,9},{9,10},{10,1... | collective-permute-start | bytes 442376 | tf_op jit(solution)/shard_map/ppermute | solution.py:29
  288.1 10.0 %collective-permute-start.36 = (bf16[48,1536]{1,0:T(8,128)(2,1)S(1)}, bf16[48,1536]{1,0:T(8,128)(2,1)S(1)}, u32[]{:S(2)}, u32[]{:S(2)}) collective-permute-start(bf16[48,1536]{1,0:T(8,128)(2,1)S(1)} %collective-permute-done.35), channel_id=1, source_target_pairs={{0,7},{1,0},{2,1},{3,2},{4,3},{5,4},{6,5},{7,6},{8,15},{9,8},{10,9... | collective-permute-start | bytes 442376 | tf_op jit(solution)/shard_map/ppermute | solution.py:29
  290.5 7.6 %collective-permute-start.39 = (bf16[48,1536]{1,0:T(8,128)(2,1)S(1)}, bf16[48,1536]{1,0:T(8,128)(2,1)S(1)}, u32[]{:S(2)}, u32[]{:S(2)}) collective-permute-start(bf16[48,1536]{1,0:T(8,128)(2,1)S(1)} %collective-permute-done.38), channel_id=1, source_target_pairs={{0,1},{1,2},{2,3},{3,4},{4,5},{5,6},{6,7},{7,0},{8,9},{9,10},{10,1... | collective-permute-start | bytes 442376 | tf_op jit(solution)/shard_map/ppermute | solution.py:29
  298.2 6.4 %collective-permute-start.40 = (bf16[48,1536]{1,0:T(8,128)(2,1)S(1)}, bf16[48,1536]{1,0:T(8,128)(2,1)S(1)}, u32[]{:S(2)}, u32[]{:S(2)}) collective-permute-start(bf16[48,1536]{1,0:T(8,128)(2,1)S(1)} %collective-permute-done.39), channel_id=1, source_target_pairs={{0,1},{1,2},{2,3},{3,4},{4,5},{5,6},{6,7},{7,0},{8,9},{9,10},{10,1... | collective-permute-start | bytes 442376 | tf_op jit(solution)/shard_map/ppermute | solution.py:29
  309.4 31.9 %copy-start.14 = (s32[3]{0:T(128)S(1)}, s32[3]{0:T(128)}, u32[]{:S(2)}) copy-start(s32[3]{0:T(128)} %param.20) | copy-start | bytes 40
  309.4 67.8 %copy-start.10 = (s32[3]{0:T(128)S(1)}, s32[3]{0:T(128)}, u32[]{:S(2)}) copy-start(s32[3]{0:T(128)} %param.18) | copy-start | bytes 40
  309.4 68.6 %copy-start.6 = (f32[48,64]{1,0:T(8,128)S(1)}, f32[48,64]{1,0:T(8,128)}, u32[]{:S(2)}) copy-start(f32[48,64]{1,0:T(8,128)} %param.16) | copy-start | bytes 36868
  309.5 12.6 %collective-permute-start.49 = (bf16[48,1536]{1,0:T(8,128)(2,1)S(1)}, bf16[48,1536]{1,0:T(8,128)(2,1)S(1)}, u32[]{:S(2)}, u32[]{:S(2)}) collective-permute-start(bf16[48,1536]{1,0:T(8,128)(2,1)S(1)} %get-tuple-element.46), channel_id=1, source_target_pairs={{0,7},{1,0},{2,1},{3,2},{4,3},{5,4},{6,5},{7,6},{8,15},{9,8},{10,9... | collective-permute-start | bytes 442376 | tf_op jit(solution)/shard_map/ppermute | solution.py:29
  309.6 13.7 %collective-permute-start.48 = (bf16[48,1536]{1,0:T(8,128)(2,1)S(1)}, bf16[48,1536]{1,0:T(8,128)(2,1)S(1)}, u32[]{:S(2)}, u32[]{:S(2)}) collective-permute-start(bf16[48,1536]{1,0:T(8,128)(2,1)S(1)} %get-tuple-element.47), channel_id=1, source_target_pairs={{0,6},{1,7},{2,0},{3,1},{4,2},{5,3},{6,4},{7,5},{8,14},{9,15},{10,... | collective-permute-start | bytes 442376 | tf_op jit(solution)/shard_map/ppermute | solution.py:29
  312.9 15.0 %collective-permute-start.47 = (bf16[48,1536]{1,0:T(8,128)(2,1)S(1)}, bf16[48,1536]{1,0:T(8,128)(2,1)S(1)}, u32[]{:S(2)}, u32[]{:S(2)}) collective-permute-start(bf16[48,1536]{1,0:T(8,128)(2,1)S(1)} %get-tuple-element.48), channel_id=1, source_target_pairs={{0,5},{1,6},{2,7},{3,0},{4,1},{5,2},{6,3},{7,4},{8,13},{9,14},{10,... | collective-permute-start | bytes 442376 | tf_op jit(solution)/shard_map/ppermute | solution.py:29
  315.6 14.3 %collective-permute-start.46 = (bf16[48,1536]{1,0:T(8,128)(2,1)S(1)}, bf16[48,1536]{1,0:T(8,128)(2,1)S(1)}, u32[]{:S(2)}, u32[]{:S(2)}) collective-permute-start(bf16[48,1536]{1,0:T(8,128)(2,1)S(1)} %get-tuple-element.49), channel_id=1, source_target_pairs={{0,4},{1,5},{2,6},{3,7},{4,0},{5,1},{6,2},{7,3},{8,12},{9,13},{10,... | collective-permute-start | bytes 442376 | tf_op jit(solution)/shard_map/ppermute | solution.py:29
  316.1 16.4 %collective-permute-start.45 = (bf16[48,1536]{1,0:T(8,128)(2,1)S(1)}, bf16[48,1536]{1,0:T(8,128)(2,1)S(1)}, u32[]{:S(2)}, u32[]{:S(2)}) collective-permute-start(bf16[48,1536]{1,0:T(8,128)(2,1)S(1)} %get-tuple-element.50), channel_id=1, source_target_pairs={{0,3},{1,4},{2,5},{3,6},{4,7},{5,0},{6,1},{7,2},{8,11},{9,12},{10,... | collective-permute-start | bytes 442376 | tf_op jit(solution)/shard_map/ppermute | solution.py:29
  322.1 16.9 %collective-permute-start.44 = (bf16[48,1536]{1,0:T(8,128)(2,1)S(1)}, bf16[48,1536]{1,0:T(8,128)(2,1)S(1)}, u32[]{:S(2)}, u32[]{:S(2)}) collective-permute-start(bf16[48,1536]{1,0:T(8,128)(2,1)S(1)} %get-tuple-element.51), channel_id=1, source_target_pairs={{0,2},{1,3},{2,4},{3,5},{4,6},{5,7},{6,0},{7,1},{8,10},{9,11},{10,... | collective-permute-start | bytes 442376 | tf_op jit(solution)/shard_map/ppermute | solution.py:29
  323.3 17.1 %collective-permute-start.43 = (bf16[48,1536]{1,0:T(8,128)(2,1)S(1)}, bf16[48,1536]{1,0:T(8,128)(2,1)S(1)}, u32[]{:S(2)}, u32[]{:S(2)}) collective-permute-start(bf16[48,1536]{1,0:T(8,128)(2,1)S(1)} %get-tuple-element.45), channel_id=1, source_target_pairs={{0,1},{1,2},{2,3},{3,4},{4,5},{5,6},{6,7},{7,0},{8,9},{9,10},{10,1... | collective-permute-start | bytes 442376 | tf_op jit(solution)/shard_map/ppermute | solution.py:29
  341.2 1.3 collective-permute-start.50
  343.1 3.6 collective-permute-start.51
  346.9 4.5 %collective-permute-start.52 = (f32[9]{0:T(128)S(1)}, f32[9]{0:T(128)S(1)}, u32[]{:S(2)}, u32[]{:S(2)}) collective-permute-start(f32[9]{0:T(128)S(1)} %pad_maximum_fusion.7), channel_id=1, source_target_pairs={{0,2},{1,3},{2,0},{3,1},{4,6},{5,7},{6,4},{7,5},{8,10},{9,11},{10,... | collective-permute-start | bytes 116 | tf_op jit(solution)/shard_map/ppermute | solution.py:24
  351.5 7.5 %collective-permute-start.53 = (f32[9]{0:T(128)S(1)}, f32[9]{0:T(128)S(1)}, u32[]{:S(2)}, u32[]{:S(2)}) collective-permute-start(f32[9]{0:T(128)S(1)} %pad_maximum_fusion.8), channel_id=1, source_target_pairs={{0,4},{1,5},{2,6},{3,7},{4,0},{5,1},{6,2},{7,3},{8,12},{9,13},{10,... | collective-permute-start | bytes 116 | tf_op jit(solution)/shard_map/ppermute | solution.py:24
  359.2 3.6 collective-permute-start.54
  362.9 5.1 %collective-permute-start.55 = (f32[9]{0:T(128)S(1)}, f32[9]{0:T(128)S(1)}, u32[]{:S(2)}, u32[]{:S(2)}) collective-permute-start(f32[9]{0:T(128)S(1)} %pad_maximum_fusion.10), channel_id=1, source_target_pairs={{0,16},{8,24},{16,0},{24,8},{32,48},{40,56},{48,32},{56,40},{64,80... | collective-permute-start | bytes 116 | tf_op jit(solution)/shard_map/ppermute | solution.py:24
  368.2 3.6 collective-permute-start.56
  371.9 5.1 %collective-permute-start.57 = (f32[9]{0:T(128)S(1)}, f32[9]{0:T(128)S(1)}, u32[]{:S(2)}, u32[]{:S(2)}) collective-permute-start(f32[9]{0:T(128)S(1)} %pad_maximum_fusion.12), channel_id=1, source_target_pairs={{0,64},{8,72},{16,80},{24,88},{32,96},{40,104},{48,112},{56,120},{... | collective-permute-start | bytes 116 | tf_op jit(solution)/shard_map/ppermute | solution.py:24
  (10 other events, 128.5 us)
Sparse Core Ops, SparseCore 0:
  76.0 63.5 all-gather.1
where the time goes:
time: 394 us; the launch traced here: 387 us
  waiting for transfers between devices  222 us (56%)
  starting transfers between devices  76.3 us (19%)
  local copies, waits for them, and re-layouts  29.8 us (8%)
  other arithmetic  16.9 us (4%)
  between operations  15.2 us (4%)
  Pallas kernels  15.1 us (4%)
  matrix products  10.9 us (3%)
    ppermute x42, waiting for transfers between devices, shifted(): lax.ppermute(value, axis, [(source, (source + step) % size) for source in...  107 us
    ppermute x42, starting transfers between devices, shifted(): lax.ppermute(value, axis, [(source, (source + step) % size) for source in...  66.8 us
    all_gather x1, waiting for transfers between devices, shards(): lax.all_gather(jnp.stack([key_rows, value_rows]), 'req', axis=1, tiled=True)  62 us
    ppermute x16, waiting for transfers between devices, swapped(): return lax.ppermute(value, axis, pairs)  53.7 us
    unnamed x80, local copies, waits for them, and re-layouts  18.3 us
    pallas_call x2, Pallas kernels, attention_sums(): pl.pallas_call(functools.partial(attention_body, head_count, head_width),...  15.1 us
    ppermute x16, starting transfers between devices, swapped(): return lax.ppermute(value, axis, pairs)  9.47 us
  transfers between devices with their start and end apart: 59, of which 44 were waited for; matrix products, arithmetic and copies ran while one was open for 4% of the time, Pallas kernels for 0%

commit v1 on v0

--- a/solution.py
+++ b/solution.py
@@ -39,22 +39,31 @@
     for unused in range((size - 1) // 2):
         backward = shifted(backward, axis, -1)
         ahead.append(backward)
-    by_offset = jnp.stack([value] + ahead + behind[::-1])
-    doubled = jnp.concatenate([by_offset, by_offset], axis=0)
-    start = (size - lax.axis_index(axis)) % size
-    ordered = lax.dynamic_slice_in_dim(doubled, start, size, axis=0)
-    return ordered.reshape((size * value.shape[0],) + value.shape[1:])
+    return jnp.concatenate([value] + ahead + behind[::-1], axis=0)
 
 
 def scatter_sum(value, axis):
     size = lax.axis_size(axis)
-    me = lax.axis_index(axis)
-    blocks = value.reshape((size, value.shape[0] // size) + value.shape[1:])
-    total = lax.dynamic_index_in_dim(blocks, me, 0, keepdims=False).astype(jnp.float32)
+    rows = value.shape[0] // size
+    total = value[:rows].astype(jnp.float32)
     for step in range(1, size):
-        outgoing = lax.dynamic_index_in_dim(blocks, (me + step) % size, 0, keepdims=False)
+        outgoing = value[step * rows : (step + 1) * rows]
         total = total + shifted(outgoing, axis, step).astype(jnp.float32)
     return total
+
+
+def offset_blocks(value, axis, to_natural):
+    size = lax.axis_size(axis)
+    me = lax.axis_index(axis)
+    blocks = value.reshape(size, value.shape[0] // size)
+    doubled = jnp.concatenate([blocks, blocks], axis=0)
+    start = (size - me) % size if to_natural else me
+    return lax.dynamic_slice_in_dim(doubled, start, size, axis=0).reshape(value.shape)
+
+
+def natural_butterfly(row_values, axis):
+    natural = offset_blocks(row_values, axis, True)
+    return offset_blocks(butterfly_sum(natural, axis), axis, False)
 
 
 def butterfly_sum(value, axis):
@@ -99,9 +108,9 @@
         den_ref[:, cols] += jnp.broadcast_to(jnp.sum(weights, axis=1, keepdims=True), (weights.shape[0], head_width))
 
 
-def attention_sums(queries, query_req, key_rows, value_rows, key_req, head_count, head_width, key_block):
+def attention_sums(queries, query_req, key_value, key_req, head_count, head_width, key_block):
     query_count, width = queries.shape
-    key_count = key_rows.shape[0]
+    key_count = key_value.shape[1]
     steps = key_count // key_block
     flops = 4 * query_count * key_count * width
     return pl.pallas_call(
@@ -109,8 +118,8 @@
         grid=(steps,),
         in_specs=[
             pl.BlockSpec((query_count, width), lambda j: (0, 0)),
-            pl.BlockSpec((key_block, width), lambda j: (j, 0)),
-            pl.BlockSpec((key_block, width), lambda j: (j, 0)),
+            pl.BlockSpec((None, key_block, width), lambda j: (0, j, 0)),
+            pl.BlockSpec((None, key_block, width), lambda j: (1, j, 0)),
             pl.BlockSpec((query_count, 1), lambda j: (0, 0)),
             pl.BlockSpec((1, key_block), lambda j: (0, j)),
         ],
@@ -127,7 +136,7 @@
             transcendentals=query_count * key_count * head_count,
             bytes_accessed=2 * (query_count + 2 * key_count) * width + 8 * query_count * width,
         ),
-    )(queries, key_rows, value_rows, query_req.reshape(query_count, 1), key_req.reshape(1, key_count))
+    )(queries, key_value, key_value, query_req.reshape(query_count, 1), key_req.reshape(1, key_count))
 
 
 def gather_project(row_block, weight):
@@ -200,7 +209,11 @@
         jnp.float32
     )
     block_first = lax.axis_index("req") * block_rows
-    query_req = request_of(block_first + jnp.arange(block_rows, dtype=jnp.int32), request_ends)
+    in_block = jnp.arange(block_rows, dtype=jnp.int32)
+    in_block = ((lax.axis_index("tp") + in_block // row_count) % tp_parts) * row_count + (
+        in_block % row_count
+    )
+    query_req = request_of(block_first + in_block, request_ends)
     head_ids = lax.axis_index("tp") * head_count + jnp.arange(head_count, dtype=jnp.int32)
     keep_cols = jnp.repeat((head_ids < HEADS).astype(jnp.float32), head_width)
     hidden_zero = states[0]
@@ -225,31 +238,37 @@
     projected = gather_project(normed, self_qkv.reshape(model_width, 3 * local_cols))
     query_raw = projected[:, :local_cols] * keep_cols
     key_raw = projected[:, local_cols : 2 * local_cols] * keep_cols
+    row_count_sums = 2 * block_rows
     norm_sums = butterfly_sum(
         jnp.concatenate(
             [
-                jnp.sum(query_raw * query_raw, axis=1),
-                jnp.sum(key_raw * key_raw, axis=1),
+                offset_blocks(
+                    jnp.stack(
+                        [jnp.sum(query_raw * query_raw, axis=1), jnp.sum(key_raw * key_raw, axis=1)],
+                        axis=1,
+                    ).reshape(-1),
+                    "tp",
+                    True,
+                ),
                 jnp.sum(text_raw * text_raw, axis=1),
             ]
         ),
         "tp",
     )
-    query_sq = norm_sums[:block_rows]
-    key_sq = norm_sums[block_rows : 2 * block_rows]
-    text_sq = norm_sums[2 * block_rows :]
+    row_sums = offset_blocks(norm_sums[:row_count_sums], "tp", False).reshape(block_rows, 2)
+    text_sq = norm_sums[row_count_sums:]
+    query_sq = row_sums[:, 0]
+    key_sq = row_sums[:, 1]
     queries = rms_scale(query_raw, query_sq, model_width, qk_gains[0])
     key_rows = rms_scale(key_raw, key_sq, model_width, qk_gains[1])
     value_rows = projected[:, 2 * local_cols :].astype(jnp.bfloat16)
     kv_all = lax.all_gather(jnp.stack([key_rows, value_rows]), "req", axis=1, tiled=True)
-    key_all = kv_all[0]
-    value_all = kv_all[1]
     key_pos = jnp.arange(all_tokens, dtype=jnp.int32)
+    key_pos = (key_pos // block_rows) * block_rows + jnp.tile(in_block, lax.axis_size("req"))
     self_num, self_den = attention_sums(
         queries,
         query_req,
-        key_all,
-        value_all,
+        kv_all,
         request_of(key_pos, request_ends),
         head_count,
         head_width,
@@ -259,7 +278,7 @@
     hidden_one = hidden_zero + gate_attn * scatter_project(self_mix, self_out)
     cross_in = (layer_norm(hidden_one) * cross_gain).astype(jnp.bfloat16)
     cross_raw = gather_project(cross_in, cross_query) * keep_cols
-    cross_sq = butterfly_sum(jnp.sum(cross_raw * cross_raw, axis=1), "tp")
+    cross_sq = natural_butterfly(jnp.sum(cross_raw * cross_raw, axis=1), "tp")
     cross_q = rms_scale(cross_raw, cross_sq, model_width, qk_gains[2])
     text_keys = rms_scale(text_raw, text_sq, model_width, qk_gains[3])
     text_values = text_local[:, 1].reshape(request_count * text_slots, local_cols)
@@ -270,7 +289,13 @@
     )
     text_req = jnp.where(text_pos < text_limit, text_req, -1)
     cross_num, cross_den = attention_sums(
-        cross_q, query_req, text_keys, text_values, text_req, head_count, head_width, text_slots
+        cross_q,
+        query_req,
+        jnp.stack([text_keys, text_values]),
+        text_req,
+        head_count,
+        head_width,
+        text_slots,
     )
     cross_mix = (cross_num / cross_den * keep_cols).astype(jnp.bfloat16)
     hidden_two = hidden_one + scatter_project(cross_mix, cross_out)

time: 394 us -> 387 us (0.982)
  waiting for transfers between devices: 222 us -> 211 us
  local copies, waits for them, and re-layouts: 29.8 us -> 19.5 us
  starting transfers between devices: 76.3 us -> 84.6 us
    ppermute x16, waiting for transfers between devices: 53.7 us -> 46.7 us  [swapped(): return lax.ppermute(value, axis, pairs)]
    squeeze x4 -> x0, local copies, waits for them, and re-layouts: 6.86 us -> none  [the longest x1 5.89 us: shards(): value_all = kv_all[1]]
    unnamed x80 -> x67, local copies, waits for them, and re-layouts: 18.3 us -> 13 us
    ppermute x16, starting transfers between devices: 9.47 us -> 13.8 us  [swapped(): return lax.ppermute(value, axis, pairs)]
    ppermute x42, waiting for transfers between devices: 107 us -> 103 us  [shifted(): lax.ppermute(value, axis, [(source, (source + step) % size) for source in...]
  transfers between devices with their start and end apart: 59 -> 59, of which waited for: 44 -> 46; matrix products, arithmetic and copies ran while one was open for 4% -> 6% of each run, Pallas kernels for 0% -> 0%
where the time goes in v1:
time: 387 us; the launch traced here: 379 us
  waiting for transfers between devices  211 us (55%)
  starting transfers between devices  84.6 us (22%)
  other arithmetic  20.5 us (5%)
  local copies, waits for them, and re-layouts  19.5 us (5%)
  Pallas kernels  15.4 us (4%)
  between operations  15 us (4%)
  matrix products  13 us (3%)
    ppermute x42, waiting for transfers between devices, shifted(): lax.ppermute(value, axis, [(source, (source + step) % size) for source in...  103 us
    ppermute x42, starting transfers between devices, shifted(): lax.ppermute(value, axis, [(source, (source + step) % size) for source in...  70.7 us
    all_gather x1, waiting for transfers between devices, shards(): lax.all_gather(jnp.stack([key_rows, value_rows]), 'req', axis=1, tiled=True)  62 us
    ppermute x16, waiting for transfers between devices, swapped(): return lax.ppermute(value, axis, pairs)  46.7 us
    pallas_call x2, Pallas kernels, attention_sums(): pl.pallas_call(functools.partial(attention_body, head_count, head_width),...  15.4 us
    ppermute x16, starting transfers between devices, swapped(): return lax.ppermute(value, axis, pairs)  13.8 us
    unnamed x67, local copies, waits for them, and re-layouts  13 us
  transfers between devices with their start and end apart: 59, of which 46 were waited for; matrix products, arithmetic and copies ran while one was open for 6% of the time, Pallas kernels for 0%

profile of v1, /device:TPU:2, one launch (start us, length us, event | category | flops | bytes accessed | tf_op | source)
XLA Modules:
  0.0 379.3 jit_solution(11700368472207907375)
XLA Ops:
  13.3 5.9 %collective-permute-start = (bf16[48,1536]{1,0:T(8,128)(2,1)S(1)}, bf16[48,1536]{1,0:T(8,128)(2,1)S(1)}, u32[]{:S(2)}, u32[]{:S(2)}) collective-permute-start(bf16[48,1536]{1,0:T(8,128)(2,1)S(1)} %get-tuple-element.40), channel_id=1, source_target_pairs={{0,7},{1,0},{2,1},{3,2},{4,3},{5,4},{6,5},{7,6},{8,15},{9,8},{10,9... | collective-permute-start | bytes 442376 | tf_op jit(solution)/shard_map/ppermute | solution.py:29
  19.1 4.3 %copy.45 = bf16[1536,3,256]{0,2,1:T(8,128)(2,1)} copy(bf16[1536,3,256]{2,0,1:T(8,128)(2,1)} %param.22) | data formatting | bytes 4718592 | tf_op args[6]
  24.9 3.3 collective-permute-start.1
  28.9 2.0 collective-permute-done.1
  30.9 3.7 collective-permute-start.2
  35.3 5.7 %collective-permute-done.5 = bf16[48,1536]{1,0:T(8,128)(2,1)S(1)} collective-permute-done((bf16[48,1536]{1,0:T(8,128)(2,1)S(1)}, bf16[48,1536]{1,0:T(8,128)(2,1)S(1)}, u32[]{:S(2)}, u32[]{:S(2)}) %collective-permute-start.5) | collective-permute-done | bytes 147488 | tf_op jit(solution)/shard_map/ppermute | solution.py:29
  41.6 5.7 %collective-permute-done.6 = bf16[48,1536]{1,0:T(8,128)(2,1)S(1)} collective-permute-done((bf16[48,1536]{1,0:T(8,128)(2,1)S(1)}, bf16[48,1536]{1,0:T(8,128)(2,1)S(1)}, u32[]{:S(2)}, u32[]{:S(2)}) %collective-permute-start.6) | collective-permute-done | bytes 147488 | tf_op jit(solution)/shard_map/ppermute | solution.py:29
  50.0 3.1 fusion.94
  54.9 3.7 collective-permute-done.7
  59.2 4.0 %collective-permute-done.8 = f32[2304]{0:T(1024)S(1)} collective-permute-done((f32[2304]{0:T(1024)S(1)}, f32[2304]{0:T(1024)S(1)}, u32[]{:S(2)}, u32[]{:S(2)}) %collective-permute-start.8) | collective-permute-done | bytes 9248 | tf_op jit(solution)/shard_map/ppermute | solution.py:24
  65.8 5.1 %collective-permute-done.9 = f32[2304]{0:T(1024)S(1)} collective-permute-done((f32[2304]{0:T(1024)S(1)}, f32[2304]{0:T(1024)S(1)}, u32[]{:S(2)}, u32[]{:S(2)}) %collective-permute-start.9) | collective-permute-done | bytes 9248 | tf_op jit(solution)/shard_map/ppermute | solution.py:24
  75.9 62.0 %all-gather.2.cloned.1.call-done.k_ref.v_ref = bf16[2,6144,256]{2,1,0:T(8,128)(2,1)} async-done(((bf16[2,384,256]{2,1,0:T(8,128)(2,1)}), bf16[2,6144,256]{2,1,0:T(8,128)(2,1)}) %all-gather.2.cloned.1.call-update) | async-done | bytes 6291472 | tf_op jit(solution)/shard_map/all_gather | solution.py:265
  137.9 10.5 %shard_map.175 = (f32[384,256]{1,0:T(8,128)}, f32[384,256]{1,0:T(8,128)}) custom-call(bf16[384,256]{1,0:T(8,128)(2,1)} %get-tuple-element.44.q_ref, bf16[2,6144,256]{2,1,0:T(8,128)(2,1)} %all-gather.2.cloned.1.call-done.k_ref.v_ref, bf16[2,6144,256]{2,1,0:T(8,128)(2,1)} %all-gather.2.cloned.1.call-done.k_ref.v_ref, s32[384,1]{1,0:T(8,128)} %reshape.366.qreq_ref, ...), custom_call_target="tpu_custom_call" | custom-call | flops 2415919104 | bytes 7274496 | tf_op jit(solution)/shard_map/pallas_call | solution.py:116
  153.5 2.6 collective-permute-start.11
  156.2 3.0 collective-permute-start.12
  159.2 2.0 collective-permute-start.13
  161.2 3.1 collective-permute-start.14
  164.4 3.4 collective-permute-start.15
  167.7 3.3 collective-permute-done.11
  174.9 4.7 %collective-permute-done.13 = bf16[48,1536]{1,0:T(8,128)(2,1)S(1)} collective-permute-done((bf16[48,1536]{1,0:T(8,128)(2,1)}, bf16[48,1536]{1,0:T(8,128)(2,1)S(1)}, u32[]{:S(2)}, u32[]{:S(2)}) %collective-permute-start.13) | collective-permute-done | bytes 147488 | tf_op jit(solution)/shard_map/ppermute | solution.py:29
  179.6 3.1 collective-permute-done.14
  182.6 3.4 collective-permute-done.15
  189.3 2.7 collective-permute-start.17
  193.8 2.2 collective-permute-done.17
  196.0 2.9 collective-permute-start.18
  199.0 2.7 collective-permute-done.18
  201.6 3.7 collective-permute-start.19
  205.8 6.3 %collective-permute-done.22 = bf16[48,1536]{1,0:T(8,128)(2,1)S(1)} collective-permute-done((bf16[48,1536]{1,0:T(8,128)(2,1)S(1)}, bf16[48,1536]{1,0:T(8,128)(2,1)S(1)}, u32[]{:S(2)}, u32[]{:S(2)}) %collective-permute-start.22) | collective-permute-done | bytes 147488 | tf_op jit(solution)/shard_map/ppermute | solution.py:29
  212.1 6.3 %collective-permute-done.23 = bf16[48,1536]{1,0:T(8,128)(2,1)S(1)} collective-permute-done((bf16[48,1536]{1,0:T(8,128)(2,1)S(1)}, bf16[48,1536]{1,0:T(8,128)(2,1)S(1)}, u32[]{:S(2)}, u32[]{:S(2)}) %collective-permute-start.23) | collective-permute-done | bytes 147488 | tf_op jit(solution)/shard_map/ppermute | solution.py:29
  219.4 3.6 collective-permute-done.24
  224.7 2.7 collective-permute-done.25
  227.4 3.0 collective-permute-start.26
  231.8 3.1 collective-permute-done.26
  235.9 4.8 %shard_map.176 = (f32[384,256]{1,0:T(8,128)}, f32[384,256]{1,0:T(8,128)}) custom-call(bf16[384,256]{1,0:T(8,128)(2,1)} %multiply_convert_fusion.2.q_ref, bf16[2,1536,256]{2,1,0:T(8,128)(2,1)} %pad_maximum_fusion.k_ref.v_ref, bf16[2,1536,256]{2,1,0:T(8,128)(2,1)} %pad_maximum_fusion.k_ref.v_ref, s32[384,1]{1,0:T(8,128)} %reshape.366.qreq_ref, ...), custom_call_target="tpu_custom_call" | custom-call | flops 603979776 | bytes 2555904 | tf_op jit(solution)/shard_map/pallas_call | solution.py:116
  243.3 3.4 collective-permute-start.29
  246.7 2.9 collective-permute-start.30
  252.8 2.3 collective-permute-start.32
  255.1 3.8 %collective-permute-done.28 = bf16[48,1536]{1,0:T(8,128)(2,1)S(1)} collective-permute-done((bf16[48,1536]{1,0:T(8,128)(2,1)S(1)}, bf16[48,1536]{1,0:T(8,128)(2,1)S(1)}, u32[]{:S(2)}, u32[]{:S(2)}) %collective-permute-start.28) | collective-permute-done | bytes 147488 | tf_op jit(solution)/shard_map/ppermute | solution.py:29
  258.9 3.2 collective-permute-done.29
  262.1 2.6 collective-permute-done.31
  264.7 3.4 collective-permute-done.32
  268.1 3.0 collective-permute-done.33
  274.6 2.5 collective-permute-done.34
  277.0 2.3 collective-permute-start.35
  279.5 3.3 collective-permute-done.35
  282.8 2.9 collective-permute-start.36
  286.0 7.6 %collective-permute-done.39 = bf16[48,1536]{1,0:T(8,128)(2,1)S(1)} collective-permute-done((bf16[48,1536]{1,0:T(8,128)(2,1)S(1)}, bf16[48,1536]{1,0:T(8,128)(2,1)S(1)}, u32[]{:S(2)}, u32[]{:S(2)}) %collective-permute-start.39) | collective-permute-done | bytes 147488 | tf_op jit(solution)/shard_map/ppermute | solution.py:29
  293.6 6.3 %collective-permute-done.40 = bf16[48,1536]{1,0:T(8,128)(2,1)S(1)} collective-permute-done((bf16[48,1536]{1,0:T(8,128)(2,1)S(1)}, bf16[48,1536]{1,0:T(8,128)(2,1)S(1)}, u32[]{:S(2)}, u32[]{:S(2)}) %collective-permute-start.40) | collective-permute-done | bytes 147488 | tf_op jit(solution)/shard_map/ppermute | solution.py:29
  300.1 2.2 fusion.17
  304.8 3.0 collective-permute-start.45
  307.8 3.4 collective-permute-start.46
  313.4 3.3 collective-permute-start.48
  316.7 5.1 %collective-permute-done.44 = bf16[48,1536]{1,0:T(8,128)(2,1)S(1)} collective-permute-done((bf16[48,1536]{1,0:T(8,128)(2,1)S(1)}, bf16[48,1536]{1,0:T(8,128)(2,1)S(1)}, u32[]{:S(2)}, u32[]{:S(2)}) %collective-permute-start.44) | collective-permute-done | bytes 147488 | tf_op jit(solution)/shard_map/ppermute | solution.py:29
  321.9 3.7 collective-permute-done.45
  326.8 4.5 %collective-permute-done.48 = bf16[48,1536]{1,0:T(8,128)(2,1)S(1)} collective-permute-done((bf16[48,1536]{1,0:T(8,128)(2,1)S(1)}, bf16[48,1536]{1,0:T(8,128)(2,1)S(1)}, u32[]{:S(2)}, u32[]{:S(2)}) %collective-permute-start.48) | collective-permute-done | bytes 147488 | tf_op jit(solution)/shard_map/ppermute | solution.py:29
  336.2 3.3 collective-permute-done.51
  340.2 4.0 %collective-permute-done.52 = f32[9]{0:T(128)S(1)} collective-permute-done((f32[9]{0:T(128)S(1)}, f32[9]{0:T(128)S(1)}, u32[]{:S(2)}, u32[]{:S(2)}) %collective-permute-start.52) | collective-permute-done | bytes 68 | tf_op jit(solution)/shard_map/ppermute | solution.py:24
  344.3 3.0 collective-permute-start.53
  347.4 4.3 %collective-permute-done.53 = f32[9]{0:T(128)S(1)} collective-permute-done((f32[9]{0:T(128)S(1)}, f32[9]{0:T(128)S(1)}, u32[]{:S(2)}, u32[]{:S(2)}) %collective-permute-start.53) | collective-permute-done | bytes 68 | tf_op jit(solution)/shard_map/ppermute | solution.py:24
  352.5 3.1 collective-permute-done.54
  357.6 3.2 collective-permute-done.55
  361.8 2.7 collective-permute-done.56
  364.7 2.1 collective-permute-start.57
  366.9 2.8 collective-permute-done.57
  (257 shorter events, 69.4 us)
Async XLA Ops:
  7.2 141.3 %copy-start = (bf16[256,1536]{1,0:T(8,128)(2,1)S(1)}, bf16[256,1536]{1,0:T(8,128)(2,1)}, u32[]{:S(2)}) copy-start(bf16[256,1536]{1,0:T(8,128)(2,1)} %param.23) | copy-start | bytes 2359300
  7.2 130.7 %all-gather.2.cloned.1.call-start = ((), (), s32[]{:S(2)}) async-start(), calls=%async_computation | async-start | bytes 6684672 | tf_op jit(solution)/shard_map/all_gather | solution.py:265
  13.3 11.7 %collective-permute-start = (bf16[48,1536]{1,0:T(8,128)(2,1)S(1)}, bf16[48,1536]{1,0:T(8,128)(2,1)S(1)}, u32[]{:S(2)}, u32[]{:S(2)}) collective-permute-start(bf16[48,1536]{1,0:T(8,128)(2,1)S(1)} %get-tuple-element.40), channel_id=1, source_target_pairs={{0,7},{1,0},{2,1},{3,2},{4,3},{5,4},{6,5},{7,6},{8,15},{9,8},{10,9... | collective-permute-start | bytes 442376 | tf_op jit(solution)/shard_map/ppermute | solution.py:29
  19.1 9.1 %collective-permute-start.3 = (bf16[48,1536]{1,0:T(8,128)(2,1)S(1)}, bf16[48,1536]{1,0:T(8,128)(2,1)S(1)}, u32[]{:S(2)}, u32[]{:S(2)}) collective-permute-start(bf16[48,1536]{1,0:T(8,128)(2,1)S(1)} %get-tuple-element.40), channel_id=1, source_target_pairs={{0,1},{1,2},{2,3},{3,4},{4,5},{5,6},{6,7},{7,0},{8,9},{9,10},{10,1... | collective-permute-start | bytes 442376 | tf_op jit(solution)/shard_map/ppermute | solution.py:29
  24.9 6.0 %collective-permute-start.1 = (bf16[48,1536]{1,0:T(8,128)(2,1)S(1)}, bf16[48,1536]{1,0:T(8,128)(2,1)S(1)}, u32[]{:S(2)}, u32[]{:S(2)}) collective-permute-start(bf16[48,1536]{1,0:T(8,128)(2,1)S(1)} %collective-permute-done), channel_id=1, source_target_pairs={{0,7},{1,0},{2,1},{3,2},{4,3},{5,4},{6,5},{7,6},{8,15},{9,8},{10,9... | collective-permute-start | bytes 442376 | tf_op jit(solution)/shard_map/ppermute | solution.py:29
  28.3 6.4 %collective-permute-start.4 = (bf16[48,1536]{1,0:T(8,128)(2,1)S(1)}, bf16[48,1536]{1,0:T(8,128)(2,1)S(1)}, u32[]{:S(2)}, u32[]{:S(2)}) collective-permute-start(bf16[48,1536]{1,0:T(8,128)(2,1)S(1)} %collective-permute-done.3), channel_id=1, source_target_pairs={{0,1},{1,2},{2,3},{3,4},{4,5},{5,6},{6,7},{7,0},{8,9},{9,10},{10,1... | collective-permute-start | bytes 442376 | tf_op jit(solution)/shard_map/ppermute | solution.py:29
  30.9 10.0 %collective-permute-start.2 = (bf16[48,1536]{1,0:T(8,128)(2,1)S(1)}, bf16[48,1536]{1,0:T(8,128)(2,1)S(1)}, u32[]{:S(2)}, u32[]{:S(2)}) collective-permute-start(bf16[48,1536]{1,0:T(8,128)(2,1)S(1)} %collective-permute-done.1), channel_id=1, source_target_pairs={{0,7},{1,0},{2,1},{3,2},{4,3},{5,4},{6,5},{7,6},{8,15},{9,8},{10,9... | collective-permute-start | bytes 442376 | tf_op jit(solution)/shard_map/ppermute | solution.py:29
  34.6 6.4 %collective-permute-start.5 = (bf16[48,1536]{1,0:T(8,128)(2,1)S(1)}, bf16[48,1536]{1,0:T(8,128)(2,1)S(1)}, u32[]{:S(2)}, u32[]{:S(2)}) collective-permute-start(bf16[48,1536]{1,0:T(8,128)(2,1)S(1)} %collective-permute-done.4), channel_id=1, source_target_pairs={{0,1},{1,2},{2,3},{3,4},{4,5},{5,6},{6,7},{7,0},{8,9},{9,10},{10,1... | collective-permute-start | bytes 442376 | tf_op jit(solution)/shard_map/ppermute | solution.py:29
  41.0 6.4 %collective-permute-start.6 = (bf16[48,1536]{1,0:T(8,128)(2,1)S(1)}, bf16[48,1536]{1,0:T(8,128)(2,1)S(1)}, u32[]{:S(2)}, u32[]{:S(2)}) collective-permute-start(bf16[48,1536]{1,0:T(8,128)(2,1)S(1)} %collective-permute-done.5), channel_id=1, source_target_pairs={{0,1},{1,2},{2,3},{3,4},{4,5},{5,6},{6,7},{7,0},{8,9},{9,10},{10,1... | collective-permute-start | bytes 442376 | tf_op jit(solution)/shard_map/ppermute | solution.py:29
  54.8 3.8 collective-permute-start.7
  58.6 4.6 %collective-permute-start.8 = (f32[2304]{0:T(1024)S(1)}, f32[2304]{0:T(1024)S(1)}, u32[]{:S(2)}, u32[]{:S(2)}) collective-permute-start(f32[2304]{0:T(1024)S(1)} %add.360), channel_id=1, source_target_pairs={{0,2},{1,3},{2,0},{3,1},{4,6},{5,7},{6,4},{7,5},{8,10},{9,11},{10,... | collective-permute-start | bytes 27656 | tf_op jit(solution)/shard_map/ppermute | solution.py:24
  63.2 7.8 %collective-permute-start.9 = (f32[2304]{0:T(1024)S(1)}, f32[2304]{0:T(1024)S(1)}, u32[]{:S(2)}, u32[]{:S(2)}) collective-permute-start(f32[2304]{0:T(1024)S(1)} %add.361), channel_id=1, source_target_pairs={{0,4},{1,5},{2,6},{3,7},{4,0},{5,1},{6,2},{7,3},{8,12},{9,13},{10,... | collective-permute-start | bytes 27656 | tf_op jit(solution)/shard_map/ppermute | solution.py:24
  151.9 12.4 %collective-permute-start.10 = (bf16[48,1536]{1,0:T(8,128)(2,1)}, bf16[48,1536]{1,0:T(8,128)(2,1)S(1)}, u32[]{:S(2)}, u32[]{:S(2)}) collective-permute-start(bf16[48,1536]{1,0:T(8,128)(2,1)} %get-tuple-element.59), channel_id=1, source_target_pairs={{0,1},{1,2},{2,3},{3,4},{4,5},{5,6},{6,7},{7,0},{8,9},{9,10},{10,1... | collective-permute-start | bytes 442376 | tf_op jit(solution)/shard_map/ppermute | solution.py:29
  153.5 17.5 %collective-permute-start.11 = (bf16[48,1536]{1,0:T(8,128)(2,1)}, bf16[48,1536]{1,0:T(8,128)(2,1)S(1)}, u32[]{:S(2)}, u32[]{:S(2)}) collective-permute-start(bf16[48,1536]{1,0:T(8,128)(2,1)} %get-tuple-element.65), channel_id=1, source_target_pairs={{0,2},{1,3},{2,4},{3,5},{4,6},{5,7},{6,0},{7,1},{8,10},{9,11},{10,... | collective-permute-start | bytes 442376 | tf_op jit(solution)/shard_map/ppermute | solution.py:29
  156.2 18.7 %collective-permute-start.12 = (bf16[48,1536]{1,0:T(8,128)(2,1)}, bf16[48,1536]{1,0:T(8,128)(2,1)S(1)}, u32[]{:S(2)}, u32[]{:S(2)}) collective-permute-start(bf16[48,1536]{1,0:T(8,128)(2,1)} %get-tuple-element.64), channel_id=1, source_target_pairs={{0,3},{1,4},{2,5},{3,6},{4,7},{5,0},{6,1},{7,2},{8,11},{9,12},{10,... | collective-permute-start | bytes 442376 | tf_op jit(solution)/shard_map/ppermute | solution.py:29
  159.2 20.4 %collective-permute-start.13 = (bf16[48,1536]{1,0:T(8,128)(2,1)}, bf16[48,1536]{1,0:T(8,128)(2,1)S(1)}, u32[]{:S(2)}, u32[]{:S(2)}) collective-permute-start(bf16[48,1536]{1,0:T(8,128)(2,1)} %get-tuple-element.63), channel_id=1, source_target_pairs={{0,4},{1,5},{2,6},{3,7},{4,0},{5,1},{6,2},{7,3},{8,12},{9,13},{10,... | collective-permute-start | bytes 442376 | tf_op jit(solution)/shard_map/ppermute | solution.py:29
  161.2 21.4 %collective-permute-start.14 = (bf16[48,1536]{1,0:T(8,128)(2,1)}, bf16[48,1536]{1,0:T(8,128)(2,1)S(1)}, u32[]{:S(2)}, u32[]{:S(2)}) collective-permute-start(bf16[48,1536]{1,0:T(8,128)(2,1)} %get-tuple-element.62), channel_id=1, source_target_pairs={{0,5},{1,6},{2,7},{3,0},{4,1},{5,2},{6,3},{7,4},{8,13},{9,14},{10,... | collective-permute-start | bytes 442376 | tf_op jit(solution)/shard_map/ppermute | solution.py:29
  164.4 21.7 %collective-permute-start.15 = (bf16[48,1536]{1,0:T(8,128)(2,1)S(1)}, bf16[48,1536]{1,0:T(8,128)(2,1)S(1)}, u32[]{:S(2)}, u32[]{:S(2)}) collective-permute-start(bf16[48,1536]{1,0:T(8,128)(2,1)S(1)} %get-tuple-element.61), channel_id=1, source_target_pairs={{0,6},{1,7},{2,0},{3,1},{4,2},{5,3},{6,4},{7,5},{8,14},{9,15},{10,... | collective-permute-start | bytes 442376 | tf_op jit(solution)/shard_map/ppermute | solution.py:29
  171.1 16.7 %collective-permute-start.16 = (bf16[48,1536]{1,0:T(8,128)(2,1)S(1)}, bf16[48,1536]{1,0:T(8,128)(2,1)S(1)}, u32[]{:S(2)}, u32[]{:S(2)}) collective-permute-start(bf16[48,1536]{1,0:T(8,128)(2,1)S(1)} %get-tuple-element.60), channel_id=1, source_target_pairs={{0,7},{1,0},{2,1},{3,2},{4,3},{5,4},{6,5},{7,6},{8,15},{9,8},{10,9... | collective-permute-start | bytes 442376 | tf_op jit(solution)/shard_map/ppermute | solution.py:29
  189.3 6.8 %collective-permute-start.17 = (bf16[48,1536]{1,0:T(8,128)(2,1)S(1)}, bf16[48,1536]{1,0:T(8,128)(2,1)S(1)}, u32[]{:S(2)}, u32[]{:S(2)}) collective-permute-start(bf16[48,1536]{1,0:T(8,128)(2,1)S(1)} %get-tuple-element.36), channel_id=1, source_target_pairs={{0,7},{1,0},{2,1},{3,2},{4,3},{5,4},{6,5},{7,6},{8,15},{9,8},{10,9... | collective-permute-start | bytes 442376 | tf_op jit(solution)/shard_map/ppermute | solution.py:29
  192.0 7.0 %collective-permute-start.20 = (bf16[48,1536]{1,0:T(8,128)(2,1)S(1)}, bf16[48,1536]{1,0:T(8,128)(2,1)S(1)}, u32[]{:S(2)}, u32[]{:S(2)}) collective-permute-start(bf16[48,1536]{1,0:T(8,128)(2,1)S(1)} %get-tuple-element.36), channel_id=1, source_target_pairs={{0,1},{1,2},{2,3},{3,4},{4,5},{5,6},{6,7},{7,0},{8,9},{9,10},{10,1... | collective-permute-start | bytes 442376 | tf_op jit(solution)/shard_map/ppermute | solution.py:29
  193.8 24.8 %copy-start.18 = (bf16[1536,256]{1,0:T(8,128)(2,1)S(1)}, bf16[1536,256]{1,0:T(8,128)(2,1)}, u32[]{:S(2)}) copy-start(bf16[1536,256]{1,0:T(8,128)(2,1)} %param.25) | copy-start | bytes 2359300
  196.0 5.6 %collective-permute-start.18 = (bf16[48,1536]{1,0:T(8,128)(2,1)S(1)}, bf16[48,1536]{1,0:T(8,128)(2,1)S(1)}, u32[]{:S(2)}, u32[]{:S(2)}) collective-permute-start(bf16[48,1536]{1,0:T(8,128)(2,1)S(1)} %collective-permute-done.17), channel_id=1, source_target_pairs={{0,7},{1,0},{2,1},{3,2},{4,3},{5,4},{6,5},{7,6},{8,15},{9,8},{10,9... | collective-permute-start | bytes 442376 | tf_op jit(solution)/shard_map/ppermute | solution.py:29
  198.9 6.4 %collective-permute-start.21 = (bf16[48,1536]{1,0:T(8,128)(2,1)S(1)}, bf16[48,1536]{1,0:T(8,128)(2,1)S(1)}, u32[]{:S(2)}, u32[]{:S(2)}) collective-permute-start(bf16[48,1536]{1,0:T(8,128)(2,1)S(1)} %collective-permute-done.20), channel_id=1, source_target_pairs={{0,1},{1,2},{2,3},{3,4},{4,5},{5,6},{6,7},{7,0},{8,9},{9,10},{10,1... | collective-permute-start | bytes 442376 | tf_op jit(solution)/shard_map/ppermute | solution.py:29
  201.6 10.5 %collective-permute-start.19 = (bf16[48,1536]{1,0:T(8,128)(2,1)S(1)}, bf16[48,1536]{1,0:T(8,128)(2,1)S(1)}, u32[]{:S(2)}, u32[]{:S(2)}) collective-permute-start(bf16[48,1536]{1,0:T(8,128)(2,1)S(1)} %collective-permute-done.18), channel_id=1, source_target_pairs={{0,7},{1,0},{2,1},{3,2},{4,3},{5,4},{6,5},{7,6},{8,15},{9,8},{10,9... | collective-permute-start | bytes 442376 | tf_op jit(solution)/shard_map/ppermute | solution.py:29
  205.3 6.8 %collective-permute-start.22 = (bf16[48,1536]{1,0:T(8,128)(2,1)S(1)}, bf16[48,1536]{1,0:T(8,128)(2,1)S(1)}, u32[]{:S(2)}, u32[]{:S(2)}) collective-permute-start(bf16[48,1536]{1,0:T(8,128)(2,1)S(1)} %collective-permute-done.21), channel_id=1, source_target_pairs={{0,1},{1,2},{2,3},{3,4},{4,5},{5,6},{6,7},{7,0},{8,9},{9,10},{10,1... | collective-permute-start | bytes 442376 | tf_op jit(solution)/shard_map/ppermute | solution.py:29
  212.1 6.4 %collective-permute-start.23 = (bf16[48,1536]{1,0:T(8,128)(2,1)S(1)}, bf16[48,1536]{1,0:T(8,128)(2,1)S(1)}, u32[]{:S(2)}, u32[]{:S(2)}) collective-permute-start(bf16[48,1536]{1,0:T(8,128)(2,1)S(1)} %collective-permute-done.22), channel_id=1, source_target_pairs={{0,1},{1,2},{2,3},{3,4},{4,5},{5,6},{6,7},{7,0},{8,9},{9,10},{10,1... | collective-permute-start | bytes 442376 | tf_op jit(solution)/shard_map/ppermute | solution.py:29
  219.3 3.6 collective-permute-start.24
  222.9 4.5 %collective-permute-start.25 = (f32[384]{0:T(512)S(1)}, f32[384]{0:T(512)S(1)}, u32[]{:S(2)}, u32[]{:S(2)}) collective-permute-start(f32[384]{0:T(512)S(1)} %add.383), channel_id=1, source_target_pairs={{0,2},{1,3},{2,0},{3,1},{4,6},{5,7},{6,4},{7,5},{8,10},{9,11},{10,... | collective-permute-start | bytes 4616 | tf_op jit(solution)/shard_map/ppermute | solution.py:24
  227.4 7.5 %collective-permute-start.26 = (f32[384]{0:T(512)S(1)}, f32[384]{0:T(512)S(1)}, u32[]{:S(2)}, u32[]{:S(2)}) collective-permute-start(f32[384]{0:T(512)S(1)} %add.384), channel_id=1, source_target_pairs={{0,4},{1,5},{2,6},{3,7},{4,0},{5,1},{6,2},{7,3},{8,12},{9,13},{10,... | collective-permute-start | bytes 4616 | tf_op jit(solution)/shard_map/ppermute | solution.py:24
  242.6 31.5 %copy-start.17 = (bf16[560,1536]{1,0:T(8,128)(2,1)S(1)}, bf16[560,1536]{1,0:T(8,128)(2,1)}, u32[]{:S(2)}) copy-start(bf16[560,1536]{1,0:T(8,128)(2,1)} %param.30) | copy-start | bytes 5160964
  242.7 10.1 %collective-permute-start.27 = (bf16[48,1536]{1,0:T(8,128)(2,1)S(1)}, bf16[48,1536]{1,0:T(8,128)(2,1)S(1)}, u32[]{:S(2)}, u32[]{:S(2)}) collective-permute-start(bf16[48,1536]{1,0:T(8,128)(2,1)S(1)} %get-tuple-element.52), channel_id=1, source_target_pairs={{0,1},{1,2},{2,3},{3,4},{4,5},{5,6},{6,7},{7,0},{8,9},{9,10},{10,1... | collective-permute-start | bytes 442376 | tf_op jit(solution)/shard_map/ppermute | solution.py:29
  242.8 16.1 %collective-permute-start.28 = (bf16[48,1536]{1,0:T(8,128)(2,1)S(1)}, bf16[48,1536]{1,0:T(8,128)(2,1)S(1)}, u32[]{:S(2)}, u32[]{:S(2)}) collective-permute-start(bf16[48,1536]{1,0:T(8,128)(2,1)S(1)} %get-tuple-element.58), channel_id=1, source_target_pairs={{0,2},{1,3},{2,4},{3,5},{4,6},{5,7},{6,0},{7,1},{8,10},{9,11},{10,... | collective-permute-start | bytes 442376 | tf_op jit(solution)/shard_map/ppermute | solution.py:29
  243.3 18.8 %collective-permute-start.29 = (bf16[48,1536]{1,0:T(8,128)(2,1)S(1)}, bf16[48,1536]{1,0:T(8,128)(2,1)S(1)}, u32[]{:S(2)}, u32[]{:S(2)}) collective-permute-start(bf16[48,1536]{1,0:T(8,128)(2,1)S(1)} %get-tuple-element.57), channel_id=1, source_target_pairs={{0,3},{1,4},{2,5},{3,6},{4,7},{5,0},{6,1},{7,2},{8,11},{9,12},{10,... | collective-permute-start | bytes 442376 | tf_op jit(solution)/shard_map/ppermute | solution.py:29
  246.7 15.4 %collective-permute-start.30 = (bf16[48,1536]{1,0:T(8,128)(2,1)S(1)}, bf16[48,1536]{1,0:T(8,128)(2,1)S(1)}, u32[]{:S(2)}, u32[]{:S(2)}) collective-permute-start(bf16[48,1536]{1,0:T(8,128)(2,1)S(1)} %get-tuple-element.56), channel_id=1, source_target_pairs={{0,4},{1,5},{2,6},{3,7},{4,0},{5,1},{6,2},{7,3},{8,12},{9,13},{10,... | collective-permute-start | bytes 442376 | tf_op jit(solution)/shard_map/ppermute | solution.py:29
  249.6 15.1 %collective-permute-start.31 = (bf16[48,1536]{1,0:T(8,128)(2,1)S(1)}, bf16[48,1536]{1,0:T(8,128)(2,1)S(1)}, u32[]{:S(2)}, u32[]{:S(2)}) collective-permute-start(bf16[48,1536]{1,0:T(8,128)(2,1)S(1)} %get-tuple-element.55), channel_id=1, source_target_pairs={{0,5},{1,6},{2,7},{3,0},{4,1},{5,2},{6,3},{7,4},{8,13},{9,14},{10,... | collective-permute-start | bytes 442376 | tf_op jit(solution)/shard_map/ppermute | solution.py:29
  252.8 15.3 %collective-permute-start.32 = (bf16[48,1536]{1,0:T(8,128)(2,1)S(1)}, bf16[48,1536]{1,0:T(8,128)(2,1)S(1)}, u32[]{:S(2)}, u32[]{:S(2)}) collective-permute-start(bf16[48,1536]{1,0:T(8,128)(2,1)S(1)} %get-tuple-element.54), channel_id=1, source_target_pairs={{0,6},{1,7},{2,0},{3,1},{4,2},{5,3},{6,4},{7,5},{8,14},{9,15},{10,... | collective-permute-start | bytes 442376 | tf_op jit(solution)/shard_map/ppermute | solution.py:29
  258.9 12.3 %collective-permute-start.33 = (bf16[48,1536]{1,0:T(8,128)(2,1)S(1)}, bf16[48,1536]{1,0:T(8,128)(2,1)S(1)}, u32[]{:S(2)}, u32[]{:S(2)}) collective-permute-start(bf16[48,1536]{1,0:T(8,128)(2,1)S(1)} %get-tuple-element.53), channel_id=1, source_target_pairs={{0,7},{1,0},{2,1},{3,2},{4,3},{5,4},{6,5},{7,6},{8,15},{9,8},{10,9... | collective-permute-start | bytes 442376 | tf_op jit(solution)/shard_map/ppermute | solution.py:29
  271.8 5.2 %collective-permute-start.34 = (bf16[48,1536]{1,0:T(8,128)(2,1)S(1)}, bf16[48,1536]{1,0:T(8,128)(2,1)S(1)}, u32[]{:S(2)}, u32[]{:S(2)}) collective-permute-start(bf16[48,1536]{1,0:T(8,128)(2,1)S(1)} %get-tuple-element.32), channel_id=1, source_target_pairs={{0,7},{1,0},{2,1},{3,2},{4,3},{5,4},{6,5},{7,6},{8,15},{9,8},{10,9... | collective-permute-start | bytes 442376 | tf_op jit(solution)/shard_map/ppermute | solution.py:29
  273.0 6.5 %collective-permute-start.37 = (bf16[48,1536]{1,0:T(8,128)(2,1)S(1)}, bf16[48,1536]{1,0:T(8,128)(2,1)S(1)}, u32[]{:S(2)}, u32[]{:S(2)}) collective-permute-start(bf16[48,1536]{1,0:T(8,128)(2,1)S(1)} %get-tuple-element.32), channel_id=1, source_target_pairs={{0,1},{1,2},{2,3},{3,4},{4,5},{5,6},{6,7},{7,0},{8,9},{9,10},{10,1... | collective-permute-start | bytes 442376 | tf_op jit(solution)/shard_map/ppermute | solution.py:29
  274.1 26.0 %collective-permute-start.41 = (bf16[560,1536]{1,0:T(8,128)(2,1)S(1)}, bf16[560,1536]{1,0:T(8,128)(2,1)S(1)}, u32[]{:S(2)}, u32[]{:S(2)}) collective-permute-start(bf16[560,1536]{1,0:T(8,128)(2,1)S(1)} %copy-done.16), channel_id=1, source_target_pairs={{0,128},{128,0},{1,129},{129,1},{2,130},{130,2},{3,131},{131,3},{4... | collective-permute-start | bytes 5160968 | tf_op jit(solution)/shard_map/ppermute | solution.py:24
  274.1 29.3 %collective-permute-start.42 = (bf16[560,1536]{1,0:T(8,128)(2,1)S(1)}, bf16[560,1536]{1,0:T(8,128)(2,1)S(1)}, u32[]{:S(2)}, u32[]{:S(2)}) collective-permute-start(bf16[560,1536]{1,0:T(8,128)(2,1)S(1)} %copy-done.17), channel_id=1, source_target_pairs={{0,128},{128,0},{1,129},{129,1},{2,130},{130,2},{3,131},{131,3},{4... | collective-permute-start | bytes 5160968 | tf_op jit(solution)/shard_map/ppermute | solution.py:24
  277.0 5.8 %collective-permute-start.35 = (bf16[48,1536]{1,0:T(8,128)(2,1)S(1)}, bf16[48,1536]{1,0:T(8,128)(2,1)S(1)}, u32[]{:S(2)}, u32[]{:S(2)}) collective-permute-start(bf16[48,1536]{1,0:T(8,128)(2,1)S(1)} %collective-permute-done.34), channel_id=1, source_target_pairs={{0,7},{1,0},{2,1},{3,2},{4,3},{5,4},{6,5},{7,6},{8,15},{9,8},{10,9... | collective-permute-start | bytes 442376 | tf_op jit(solution)/shard_map/ppermute | solution.py:29
  279.5 6.5 %collective-permute-start.38 = (bf16[48,1536]{1,0:T(8,128)(2,1)S(1)}, bf16[48,1536]{1,0:T(8,128)(2,1)S(1)}, u32[]{:S(2)}, u32[]{:S(2)}) collective-permute-start(bf16[48,1536]{1,0:T(8,128)(2,1)S(1)} %collective-permute-done.37), channel_id=1, source_target_pairs={{0,1},{1,2},{2,3},{3,4},{4,5},{5,6},{6,7},{7,0},{8,9},{9,10},{10,1... | collective-permute-start | bytes 442376 | tf_op jit(solution)/shard_map/ppermute | solution.py:29
  282.8 10.8 %collective-permute-start.36 = (bf16[48,1536]{1,0:T(8,128)(2,1)S(1)}, bf16[48,1536]{1,0:T(8,128)(2,1)S(1)}, u32[]{:S(2)}, u32[]{:S(2)}) collective-permute-start(bf16[48,1536]{1,0:T(8,128)(2,1)S(1)} %collective-permute-done.35), channel_id=1, source_target_pairs={{0,7},{1,0},{2,1},{3,2},{4,3},{5,4},{6,5},{7,6},{8,15},{9,8},{10,9... | collective-permute-start | bytes 442376 | tf_op jit(solution)/shard_map/ppermute | solution.py:29
  286.0 7.6 %collective-permute-start.39 = (bf16[48,1536]{1,0:T(8,128)(2,1)S(1)}, bf16[48,1536]{1,0:T(8,128)(2,1)S(1)}, u32[]{:S(2)}, u32[]{:S(2)}) collective-permute-start(bf16[48,1536]{1,0:T(8,128)(2,1)S(1)} %collective-permute-done.38), channel_id=1, source_target_pairs={{0,1},{1,2},{2,3},{3,4},{4,5},{5,6},{6,7},{7,0},{8,9},{9,10},{10,1... | collective-permute-start | bytes 442376 | tf_op jit(solution)/shard_map/ppermute | solution.py:29
  293.6 6.4 %collective-permute-start.40 = (bf16[48,1536]{1,0:T(8,128)(2,1)S(1)}, bf16[48,1536]{1,0:T(8,128)(2,1)S(1)}, u32[]{:S(2)}, u32[]{:S(2)}) collective-permute-start(bf16[48,1536]{1,0:T(8,128)(2,1)S(1)} %collective-permute-done.39), channel_id=1, source_target_pairs={{0,1},{1,2},{2,3},{3,4},{4,5},{5,6},{6,7},{7,0},{8,9},{9,10},{10,1... | collective-permute-start | bytes 442376 | tf_op jit(solution)/shard_map/ppermute | solution.py:29
  304.6 8.8 %collective-permute-start.43 = (bf16[48,1536]{1,0:T(8,128)(2,1)S(1)}, bf16[48,1536]{1,0:T(8,128)(2,1)S(1)}, u32[]{:S(2)}, u32[]{:S(2)}) collective-permute-start(bf16[48,1536]{1,0:T(8,128)(2,1)S(1)} %get-tuple-element.45), channel_id=1, source_target_pairs={{0,1},{1,2},{2,3},{3,4},{4,5},{5,6},{6,7},{7,0},{8,9},{9,10},{10,1... | collective-permute-start | bytes 442376 | tf_op jit(solution)/shard_map/ppermute | solution.py:29
  304.7 17.1 %collective-permute-start.44 = (bf16[48,1536]{1,0:T(8,128)(2,1)S(1)}, bf16[48,1536]{1,0:T(8,128)(2,1)S(1)}, u32[]{:S(2)}, u32[]{:S(2)}) collective-permute-start(bf16[48,1536]{1,0:T(8,128)(2,1)S(1)} %get-tuple-element.51), channel_id=1, source_target_pairs={{0,2},{1,3},{2,4},{3,5},{4,6},{5,7},{6,0},{7,1},{8,10},{9,11},{10,... | collective-permute-start | bytes 442376 | tf_op jit(solution)/shard_map/ppermute | solution.py:29
  304.8 20.8 %collective-permute-start.45 = (bf16[48,1536]{1,0:T(8,128)(2,1)S(1)}, bf16[48,1536]{1,0:T(8,128)(2,1)S(1)}, u32[]{:S(2)}, u32[]{:S(2)}) collective-permute-start(bf16[48,1536]{1,0:T(8,128)(2,1)S(1)} %get-tuple-element.50), channel_id=1, source_target_pairs={{0,3},{1,4},{2,5},{3,6},{4,7},{5,0},{6,1},{7,2},{8,11},{9,12},{10,... | collective-permute-start | bytes 442376 | tf_op jit(solution)/shard_map/ppermute | solution.py:29
  307.8 17.8 %collective-permute-start.46 = (bf16[48,1536]{1,0:T(8,128)(2,1)S(1)}, bf16[48,1536]{1,0:T(8,128)(2,1)S(1)}, u32[]{:S(2)}, u32[]{:S(2)}) collective-permute-start(bf16[48,1536]{1,0:T(8,128)(2,1)S(1)} %get-tuple-element.49), channel_id=1, source_target_pairs={{0,4},{1,5},{2,6},{3,7},{4,0},{5,1},{6,2},{7,3},{8,12},{9,13},{10,... | collective-permute-start | bytes 442376 | tf_op jit(solution)/shard_map/ppermute | solution.py:29
  311.2 15.6 %collective-permute-start.47 = (bf16[48,1536]{1,0:T(8,128)(2,1)S(1)}, bf16[48,1536]{1,0:T(8,128)(2,1)S(1)}, u32[]{:S(2)}, u32[]{:S(2)}) collective-permute-start(bf16[48,1536]{1,0:T(8,128)(2,1)S(1)} %get-tuple-element.48), channel_id=1, source_target_pairs={{0,5},{1,6},{2,7},{3,0},{4,1},{5,2},{6,3},{7,4},{8,13},{9,14},{10,... | collective-permute-start | bytes 442376 | tf_op jit(solution)/shard_map/ppermute | solution.py:29
  313.4 17.9 %collective-permute-start.48 = (bf16[48,1536]{1,0:T(8,128)(2,1)S(1)}, bf16[48,1536]{1,0:T(8,128)(2,1)S(1)}, u32[]{:S(2)}, u32[]{:S(2)}) collective-permute-start(bf16[48,1536]{1,0:T(8,128)(2,1)S(1)} %get-tuple-element.47), channel_id=1, source_target_pairs={{0,6},{1,7},{2,0},{3,1},{4,2},{5,3},{6,4},{7,5},{8,14},{9,15},{10,... | collective-permute-start | bytes 442376 | tf_op jit(solution)/shard_map/ppermute | solution.py:29
  321.8 48.2 %copy-start.15 = (s32[3]{0:T(128)S(1)}, s32[3]{0:T(128)}, u32[]{:S(2)}) copy-start(s32[3]{0:T(128)} %param.18) | copy-start | bytes 40
  321.8 49.0 %copy-start.7 = (f32[48,64]{1,0:T(8,128)S(1)}, f32[48,64]{1,0:T(8,128)}, u32[]{:S(2)}) copy-start(f32[48,64]{1,0:T(8,128)} %param.16) | copy-start | bytes 36868
  321.8 11.4 %collective-permute-start.49 = (bf16[48,1536]{1,0:T(8,128)(2,1)S(1)}, bf16[48,1536]{1,0:T(8,128)(2,1)S(1)}, u32[]{:S(2)}, u32[]{:S(2)}) collective-permute-start(bf16[48,1536]{1,0:T(8,128)(2,1)S(1)} %get-tuple-element.46), channel_id=1, source_target_pairs={{0,7},{1,0},{2,1},{3,2},{4,3},{5,4},{6,5},{7,6},{8,15},{9,8},{10,9... | collective-permute-start | bytes 442376 | tf_op jit(solution)/shard_map/ppermute | solution.py:29
  334.0 1.3 collective-permute-start.50
  335.9 3.6 collective-permute-start.51
  339.7 4.5 %collective-permute-start.52 = (f32[9]{0:T(128)S(1)}, f32[9]{0:T(128)S(1)}, u32[]{:S(2)}, u32[]{:S(2)}) collective-permute-start(f32[9]{0:T(128)S(1)} %pad_maximum_fusion.8), channel_id=1, source_target_pairs={{0,2},{1,3},{2,0},{3,1},{4,6},{5,7},{6,4},{7,5},{8,10},{9,11},{10,... | collective-permute-start | bytes 116 | tf_op jit(solution)/shard_map/ppermute | solution.py:24
  344.3 7.5 %collective-permute-start.53 = (f32[9]{0:T(128)S(1)}, f32[9]{0:T(128)S(1)}, u32[]{:S(2)}, u32[]{:S(2)}) collective-permute-start(f32[9]{0:T(128)S(1)} %pad_maximum_fusion.9), channel_id=1, source_target_pairs={{0,4},{1,5},{2,6},{3,7},{4,0},{5,1},{6,2},{7,3},{8,12},{9,13},{10,... | collective-permute-start | bytes 116 | tf_op jit(solution)/shard_map/ppermute | solution.py:24
  352.0 3.6 collective-permute-start.54
  355.7 5.1 %collective-permute-start.55 = (f32[9]{0:T(128)S(1)}, f32[9]{0:T(128)S(1)}, u32[]{:S(2)}, u32[]{:S(2)}) collective-permute-start(f32[9]{0:T(128)S(1)} %pad_maximum_fusion.11), channel_id=1, source_target_pairs={{0,16},{8,24},{16,0},{24,8},{32,48},{40,56},{48,32},{56,40},{64,80... | collective-permute-start | bytes 116 | tf_op jit(solution)/shard_map/ppermute | solution.py:24
  360.9 3.6 collective-permute-start.56
  364.7 5.1 %collective-permute-start.57 = (f32[9]{0:T(128)S(1)}, f32[9]{0:T(128)S(1)}, u32[]{:S(2)}, u32[]{:S(2)}) collective-permute-start(f32[9]{0:T(128)S(1)} %pad_maximum_fusion.13), channel_id=1, source_target_pairs={{0,64},{8,72},{16,80},{24,88},{32,96},{40,104},{48,112},{56,120},{... | collective-permute-start | bytes 116 | tf_op jit(solution)/shard_map/ppermute | solution.py:24
  (15 other events, 107.9 us)
Sparse Core Ops, SparseCore 0:
  74.3 63.5 all-gather.1
